TPU v7x, 128 devices: a whole 4x4x4 slice. The times are simulated.
128 devices in a mesh: blk: 64 (over z_lo, x, y, core), rep: 2 (over z_hi).
Axes of the slice: x: 4, y: 4, z: 4 (z_hi: 2, z_lo: 2; z = z_hi * 2 + z_lo), core: 2. Of those that a mesh axis runs over, the one named last changes fastest.
Arguments:
- features: bfloat16 [65536, 256], P('blk'), may hold values from -6 to 6
- weight: bfloat16 [256, 256], replicated, may hold values from -0.375 to 0.375
- bias: float32 [256], replicated, may hold values from -3 to 3
- cotangent: bfloat16 [65536, 256], P('blk'), may hold values from -6 to 6
- train_mask: int32 [65536], P('blk'), may hold values 0 or 1
- tile_cols: int32 [512, 16], P('blk', 'rep'), may hold values from -1 to 511, as said below
- tile_values: bfloat16 [512, 16, 128, 128], P('blk', 'rep'), as said below
Outputs:
- output: bfloat16 [65536, 256], P('blk')
- grad_in: bfloat16 [65536, 256], P('blk')
Inputs may be any that keep to these rules, and one draw needn't show every extreme that they name: `tile_cols`: the live slots of a row tile name distinct column tiles, each in a slab at most 2 slabs from the row tile's slab around the loop of slabs (the last slab beside the first). In each half of a row tile's 16 slots (the first and the last 8) the live slots come first; some half of some row tile is full in every draw. `tile_values`: Nonnegative; the tile of an empty slot is all zeros.
All inputs are finite; a program needn't handle non-finite values. No bound on the sum of `train_mask` on one device may be relied on, other than what follows from the above.
Results may differ from a plain program's by a relative error of at most 0.0062.
Values may be sent and summed in bfloat16 or wider, within the bound.
No kernel may reach another device: no remote copies, remote signals or barrier semaphores. Data moves between devices by JAX's collectives and lax.ppermute only.
A program may use at most 64 MiB of HBM per device.

v0:
```python
import jax
import jax.numpy as jnp
from jax import lax
from jax.sharding import PartitionSpec as P

REACH = 2


def passed_along(array, axis, by):
    count = lax.axis_size(axis)
    return lax.ppermute(array, axis, [(i, (i + by) % count) for i in range(count)])


def silu_grad(preact):
    sigmoid_z = jax.nn.sigmoid(preact)
    return sigmoid_z * (1.0 + preact * (1.0 - sigmoid_z))


def activate(preact, mask_rows, cot_rows):
    output = jax.nn.silu(preact).astype(jnp.bfloat16)
    scaled = (
        mask_rows.astype(jnp.float32)[:, None] * cot_rows.astype(jnp.float32) * silu_grad(preact)
    ).astype(jnp.bfloat16)
    return (output, scaled)


def shards(features, weight, bias, cotangent, train_mask, tile_cols, tile_values):
    row_count, feat_width = features.shape
    tile_size = tile_values.shape[2]
    row_tiles = row_count // tile_size
    loop_size = lax.axis_size("blk")
    position = lax.axis_index("blk")
    span = 2 * REACH + 1
    projected = jnp.dot(features, weight, preferred_element_type=jnp.float32).astype(jnp.bfloat16)
    above = []
    below = []
    for direction in (1, -1):
        moving = projected
        collected = []
        for distance in range(REACH):
            moving = passed_along(moving, "blk", -direction)
            collected.append(moving)
        if direction == 1:
            above = collected
        else:
            below = collected
    window = jnp.concatenate(below[::-1] + [projected] + above, axis=0)
    window_tiles = window.reshape(span * row_tiles, tile_size, feat_width)
    live_mask = tile_cols >= 0
    offset = jnp.mod(tile_cols // row_tiles - position + REACH, loop_size)
    local_index = jnp.where(live_mask, offset * row_tiles + tile_cols % row_tiles, 0)
    target = jnp.where(live_mask, local_index, span * row_tiles)
    rounds = 1

    def forward_round(round_index, running):
        gathered = window_tiles[local_index]
        return running + jnp.einsum(
            "rsij,rsjf->rif", tile_values, gathered, preferred_element_type=jnp.float32
        )

    partial_value = lax.fori_loop(
        0, rounds, forward_round, jnp.zeros((row_tiles, tile_size, feat_width), jnp.float32)
    )
    partial_value = partial_value.reshape(row_count, feat_width)
    preact = lax.psum(partial_value, "rep") + bias
    output, scaled = activate(preact, train_mask, cotangent)
    scaled_tiles = scaled.reshape(row_tiles, tile_size, feat_width)

    def backward_round(round_index, running):
        products = jnp.einsum(
            "rsij,rif->rsjf", tile_values, scaled_tiles, preferred_element_type=jnp.float32
        )
        return running + jax.ops.segment_sum(
            products.reshape(-1, tile_size, feat_width),
            target.reshape(-1),
            num_segments=span * row_tiles,
        )

    pieces = lax.fori_loop(
        0, rounds, backward_round, jnp.zeros((span * row_tiles, tile_size, feat_width), jnp.float32)
    )
    pieces = pieces.reshape(span, row_count, feat_width)
    gathered_sum = pieces[REACH]
    for direction in (1, -1):
        carried = jnp.zeros((row_count, feat_width), jnp.float32)
        for distance in range(REACH, 0, -1):
            carried = passed_along(carried + pieces[REACH + direction * distance], "blk", direction)
        gathered_sum = gathered_sum + carried
    back_sum = lax.psum(gathered_sum, "rep").astype(jnp.bfloat16)
    grad_in = jnp.dot(back_sum, weight.T, preferred_element_type=jnp.float32).astype(jnp.bfloat16)
    return (output, grad_in)


def solution(mesh):
    placed = (
        P("blk", None),
        P(),
        P(),
        P("blk", None),
        P("blk"),
        P("blk", "rep"),
        P("blk", "rep", None, None),
    )
    return jax.shard_map(
        shards,
        mesh=mesh,
        in_specs=placed,
        out_specs=(P("blk", None), P("blk", None)),
        check_vma=False,
    )
```

profile of v0, /device:TPU:31, one launch (start us, length us, event | category | flops | bytes accessed | tf_op | source)
XLA Modules:
  0.0 209.3 jit_solution(11464197328930705412)
XLA Ops:
  7.2 0.0 copy-start
  7.2 0.0 all-reduce.3.cloned.1.call-start
  7.2 1.5 convolution_convert_fusion.1
  8.7 1.8 collective-permute-start
  10.6 0.0 collective-permute-start.2
  10.6 6.1 %collective-permute-done = bf16[1024,256]{1,0:T(8,128)(2,1)} collective-permute-done((bf16[1024,256]{1,0:T(8,128)(2,1)S(1)}, bf16[1024,256]{1,0:T(8,128)(2,1)}, u32[]{:S(2)}, u32[]{:S(2)}) %collective-permute-start) | collective-permute-done | bytes 524320 | tf_op jit(solution)/shard_map/ppermute | solution.py:11
  16.7 6.8 %collective-permute-start.1 = (bf16[1024,256]{1,0:T(8,128)(2,1)}, bf16[1024,256]{1,0:T(8,128)(2,1)}, u32[]{:S(2)}, u32[]{:S(2)}) collective-permute-start(bf16[1024,256]{1,0:T(8,128)(2,1)} %collective-permute-done), channel_id=1, source_target_pairs={{0,2},{2,4},{4,6},{6,8},{8,10},{10,12},{12,14},{14,16},{16,18},{18... | collective-permute-start | bytes 1572872 | tf_op jit(solution)/shard_map/ppermute | solution.py:11
  23.5 0.7 broadcast_select_fusion
  24.2 0.1 reshape.41
  24.3 0.0 collective-permute-done.2
  24.3 0.1 collective-permute-start.3
  24.4 5.6 %collective-permute-done.1 = bf16[1024,256]{1,0:T(8,128)(2,1)} collective-permute-done((bf16[1024,256]{1,0:T(8,128)(2,1)}, bf16[1024,256]{1,0:T(8,128)(2,1)}, u32[]{:S(2)}, u32[]{:S(2)}) %collective-permute-start.1) | collective-permute-done | bytes 524320 | tf_op jit(solution)/shard_map/ppermute | solution.py:11
  29.9 1.9 constant_dynamic-update-slice_fusion.4
  31.8 1.9 constant_dynamic-update-slice_fusion.3
  33.7 0.9 constant_dynamic-update-slice_fusion.2
  34.6 0.8 constant_dynamic-update-slice_fusion.1
  35.4 1.8 collective-permute-done.3
  37.2 0.9 constant_dynamic-update-slice_fusion
  38.0 4.5 %gather_fusion = bf16[64,128,256]{2,1,0:T(8,128)(2,1)} fusion(bf16[40,128,256]{2,1,0:T(8,128)(2,1)} %bitcast, s32[1024]{0:T(1024)S(1)} %pad_clamp_fusion), kind=kCustom, calls=%fused_computation | custom fusion | bytes 8388864 | tf_op jit(solution)/shard_map/while/body/eval_jaxpr/gather | solution.py:56
  42.5 0.0 copy-done
  42.5 0.0 copy-start.3
  42.6 4.0 %fusion.11 = f32[8,256,128,1]{1,2,3,0:T(8,128)} fusion(bf16[8,8,128,128]{3,2,1,0:T(8,128)(2,1)S(1)} %copy-done, bf16[8,8,128,256]{3,2,1,0:T(8,128)(2,1)} %bitcast.35), kind=kOutput, calls=%fused_computation.39 | convolution fusion | flops 536870912 | bytes 7340032 | tf_op jit(solution)/shard_map/while/body/eval_jaxpr/rsij,rsjf->rif/dot_general | solution.py:57
  46.6 0.0 all-reduce.3.cloned.1.call-update
  46.6 0.0 copy-done.3
  46.6 0.1 reshape.49
  46.7 48.9 %all-reduce.3.cloned.1.call-done = f32[1024,256]{1,0:T(8,128)} async-done(((f32[1024,256]{1,0:T(8,128)}), f32[1024,256]{1,0:T(8,128)}) %all-reduce.3.cloned.1.call-update) | async-done | bytes 1048592 | tf_op jit(solution)/shard_map/psum | solution.py:65
  95.6 0.0 copy-done.1
  95.6 0.0 copy-done.4
  95.6 2.5 %multiply_convert_fusion = (bf16[1024,256]{1,0:T(8,128)(2,1)S(1)}, bf16[1024,256]{1,0:T(8,128)(2,1)}) fusion(bf16[1024,256]{1,0:T(8,128)(2,1)S(1)} %copy-done.1, f32[1024,256]{1,0:T(8,128)} %all-reduce.3.cloned.1.call-done, f32[1024]{0:T(1024)S(1)} %convert_element_type.23, f32[256]{0:T(256)S(1)} %copy-done.4), kind=kLoop, calls=%fused_computation.8 | loop fusion | flops 3670016 | bytes 2626560 | tf_op jit(solution)/shard_map/convert_element_type | solution.py:23
  98.1 4.5 %fusion.10 = f32[8,256,8,128]{3,1,2,0:T(8,128)} fusion(bf16[8,128,256,1]{2,1,3,0:T(8,128)(2,1)S(1)} %bitcast.37, bf16[8,8,128,128]{3,2,1,0:T(8,128)(2,1)S(1)} %copy-done), kind=kOutput, calls=%fused_computation.38 | convolution fusion | flops 536870912 | bytes 11010048 | tf_op jit(solution)/shard_map/while/body/eval_jaxpr/rsij,rif->rsjf/dot_general | solution.py:70
  102.6 9.0 %copy.11 = f32[64,128,256]{2,1,0:T(8,128)} copy(f32[64,128,256]{1,2,0:T(8,128)} %bitcast.34) | data formatting | bytes 16777216 | tf_op jit(solution)/shard_map/while/body/eval_jaxpr/reshape | solution.py:74
  111.6 3.0 %broadcast.33 = f32[40,128,256]{2,1,0:T(8,128)} broadcast(f32[]{:T(128)} %constant.70.clone.1), dimensions={} | broadcast | bytes 5242884 | tf_op jit(solution)/shard_map/broadcast.13
  114.6 19.2 %scatter_fusion = f32[40,128,256]{2,1,0:T(8,128)} fusion(f32[40,128,256]{2,1,0:T(8,128)} %broadcast.33, s32[64]{0:T(128)S(1)} %reshape.49, f32[64,128,256]{2,1,0:T(8,128)} %copy.11), kind=kCustom, calls=%fused_computation.1 | custom fusion | flops 2097152 | bytes 25166080 | tf_op jit(solution)/shard_map/while/body/eval_jaxpr/scatter-add | solution.py:73
  133.8 2.8 %fusion.9 = (f32[8,128,256]{2,1,0:T(8,128)S(1)}, f32[8,128,256]{2,1,0:T(8,128)S(1)}, f32[8,128,256]{2,1,0:T(8,128)S(1)}, f32[8,128,256]{2,1,0:T(8,128)S(1)}, f32[8,128,256]{2,1,0:T(8,128)S(1)}) fusion(f32[40,128,256]{2,1,0:T(8,128)} %scatter_fusion), kind=kLoop, calls=%fused_computation.37 | loop fusion | bytes 10485760 | tf_op jit(solution)/shard_map/slice | solution.py:83
  136.6 0.8 collective-permute-start.4
  137.5 0.0 collective-permute-start.6
  137.5 11.7 %collective-permute-done.4 = f32[1024,256]{1,0:T(8,128)S(1)} collective-permute-done((f32[1024,256]{1,0:T(8,128)S(1)}, f32[1024,256]{1,0:T(8,128)S(1)}, u32[]{:S(2)}, u32[]{:S(2)}) %collective-permute-start.4) | collective-permute-done | bytes 1048608 | tf_op jit(solution)/shard_map/ppermute | solution.py:11
  149.2 0.1 bitcast_add_fusion.1
  149.4 6.8 %collective-permute-start.5 = (f32[1024,256]{1,0:T(8,128)S(1)}, f32[1024,256]{1,0:T(8,128)S(1)}, u32[]{:S(2)}, u32[]{:S(2)}) collective-permute-start(f32[1024,256]{1,0:T(8,128)S(1)} %bitcast_add_fusion.1), channel_id=1, source_target_pairs={{0,2},{2,4},{4,6},{6,8},{8,10},{10,12},{12,14},{14,16},{16,18},{18... | collective-permute-start | bytes 3145736 | tf_op jit(solution)/shard_map/ppermute | solution.py:11
  156.1 0.0 collective-permute-done.6
  156.1 0.1 bitcast_add_fusion
  156.3 0.1 collective-permute-start.7
  156.3 11.5 %collective-permute-done.5 = f32[1024,256]{1,0:T(8,128)S(1)} collective-permute-done((f32[1024,256]{1,0:T(8,128)S(1)}, f32[1024,256]{1,0:T(8,128)S(1)}, u32[]{:S(2)}, u32[]{:S(2)}) %collective-permute-start.5) | collective-permute-done | bytes 1048608 | tf_op jit(solution)/shard_map/ppermute | solution.py:11
  167.9 7.0 %collective-permute-done.7 = f32[1024,256]{1,0:T(8,128)S(1)} collective-permute-done((f32[1024,256]{1,0:T(8,128)S(1)}, f32[1024,256]{1,0:T(8,128)S(1)}, u32[]{:S(2)}, u32[]{:S(2)}) %collective-permute-start.7) | collective-permute-done | bytes 1048608 | tf_op jit(solution)/shard_map/ppermute | solution.py:11
  174.9 0.2 fusion
  175.1 25.2 %all-reduce.4 = bf16[1024,256]{1,0:T(8,128)(2,1)} all-reduce(f32[1024,256]{1,0:T(8,128)S(1)} %fusion), channel_id=1, replica_groups=mesh['blk'=64,'rep'=2] {'rep'}, use_global_device_ids=true, to_apply=%region_2.3 | all-reduce | flops 262144 | bytes 1572864 | tf_op jit(solution)/shard_map/psum | solution.py:89
  200.3 0.0 copy-done.2
  200.3 2.2 %convolution_convert_fusion = bf16[1024,256]{1,0:T(8,128)(2,1)} fusion(bf16[256,256]{1,0:T(8,128)(2,1)S(1)} %copy-done.2, bf16[1024,256]{1,0:T(8,128)(2,1)} %all-reduce.4), kind=kOutput, calls=%fused_computation.2 | convolution fusion | flops 134479872 | bytes 1179648 | tf_op jit(solution)/shard_map/dot_general | solution.py:90
  (5 shorter events, 0.0 us)
Async XLA Ops:
  7.2 35.4 %copy-start = (bf16[8,8,128,128]{3,2,1,0:T(8,128)(2,1)S(1)}, bf16[8,8,128,128]{3,2,1,0:T(8,128)(2,1)}, u32[]{:S(2)}) copy-start(bf16[8,8,128,128]{3,2,1,0:T(8,128)(2,1)} %param.13) | copy-start | bytes 6291460
  7.2 88.4 %all-reduce.3.cloned.1.call-start = ((), (), s32[]{:S(2)}) async-start(), calls=%async_computation | async-start | bytes 2097152 | tf_op jit(solution)/shard_map/psum | solution.py:65
  8.7 8.0 %collective-permute-start = (bf16[1024,256]{1,0:T(8,128)(2,1)S(1)}, bf16[1024,256]{1,0:T(8,128)(2,1)}, u32[]{:S(2)}, u32[]{:S(2)}) collective-permute-start(bf16[1024,256]{1,0:T(8,128)(2,1)S(1)} %convolution_convert_fusion.1), channel_id=1, source_target_pairs={{0,2},{2,4},{4,6},{6,8},{8,10},{10,12},{12,14},{14,16},{16,18},{18... | collective-permute-start | bytes 1572872 | tf_op jit(solution)/shard_map/ppermute | solution.py:11
  10.6 13.7 %collective-permute-start.2 = (bf16[1024,256]{1,0:T(8,128)(2,1)S(1)}, bf16[1024,256]{1,0:T(8,128)(2,1)S(1)}, u32[]{:S(2)}, u32[]{:S(2)}) collective-permute-start(bf16[1024,256]{1,0:T(8,128)(2,1)S(1)} %convolution_convert_fusion.1), channel_id=1, source_target_pairs={{0,126},{2,0},{4,2},{6,4},{8,6},{10,8},{12,10},{14,12},{16,14},{18... | collective-permute-start | bytes 1572872 | tf_op jit(solution)/shard_map/ppermute | solution.py:11
  16.7 13.2 %collective-permute-start.1 = (bf16[1024,256]{1,0:T(8,128)(2,1)}, bf16[1024,256]{1,0:T(8,128)(2,1)}, u32[]{:S(2)}, u32[]{:S(2)}) collective-permute-start(bf16[1024,256]{1,0:T(8,128)(2,1)} %collective-permute-done), channel_id=1, source_target_pairs={{0,2},{2,4},{4,6},{6,8},{8,10},{10,12},{12,14},{14,16},{16,18},{18... | collective-permute-start | bytes 1572872 | tf_op jit(solution)/shard_map/ppermute | solution.py:11
  24.3 12.9 %collective-permute-start.3 = (bf16[1024,256]{1,0:T(8,128)(2,1)S(1)}, bf16[1024,256]{1,0:T(8,128)(2,1)S(1)}, u32[]{:S(2)}, u32[]{:S(2)}) collective-permute-start(bf16[1024,256]{1,0:T(8,128)(2,1)S(1)} %collective-permute-done.2), channel_id=1, source_target_pairs={{0,126},{2,0},{4,2},{6,4},{8,6},{10,8},{12,10},{14,12},{16,14},{18... | collective-permute-start | bytes 1572872 | tf_op jit(solution)/shard_map/ppermute | solution.py:11
  42.5 4.1 %copy-start.3 = (s32[1024]{0:T(1024)S(1)}, s32[1024]{0:T(1024)}, u32[]{:S(2)}) copy-start(s32[1024]{0:T(1024)} %param.11) | copy-start | bytes 12292
  42.5 53.0 %copy-start.1 = (bf16[1024,256]{1,0:T(8,128)(2,1)S(1)}, bf16[1024,256]{1,0:T(8,128)(2,1)}, u32[]{:S(2)}) copy-start(bf16[1024,256]{1,0:T(8,128)(2,1)} %param.10) | copy-start | bytes 1572868
  42.5 53.0 %copy-start.4 = (f32[256]{0:T(256)S(1)}, f32[256]{0:T(256)}, u32[]{:S(2)}) copy-start(f32[256]{0:T(256)} %param.9) | copy-start | bytes 3076
  136.6 12.6 %collective-permute-start.4 = (f32[1024,256]{1,0:T(8,128)S(1)}, f32[1024,256]{1,0:T(8,128)S(1)}, u32[]{:S(2)}, u32[]{:S(2)}) collective-permute-start(f32[1024,256]{1,0:T(8,128)S(1)} %bitcast.39), channel_id=1, source_target_pairs={{0,2},{2,4},{4,6},{6,8},{8,10},{10,12},{12,14},{14,16},{16,18},{18... | collective-permute-start | bytes 3145736 | tf_op jit(solution)/shard_map/ppermute | solution.py:11
  137.5 18.7 %collective-permute-start.6 = (f32[1024,256]{1,0:T(8,128)S(1)}, f32[1024,256]{1,0:T(8,128)S(1)}, u32[]{:S(2)}, u32[]{:S(2)}) collective-permute-start(f32[1024,256]{1,0:T(8,128)S(1)} %bitcast.38), channel_id=1, source_target_pairs={{0,126},{2,0},{4,2},{6,4},{8,6},{10,8},{12,10},{14,12},{16,14},{18... | collective-permute-start | bytes 3145736 | tf_op jit(solution)/shard_map/ppermute | solution.py:11
  149.4 18.5 %collective-permute-start.5 = (f32[1024,256]{1,0:T(8,128)S(1)}, f32[1024,256]{1,0:T(8,128)S(1)}, u32[]{:S(2)}, u32[]{:S(2)}) collective-permute-start(f32[1024,256]{1,0:T(8,128)S(1)} %bitcast_add_fusion.1), channel_id=1, source_target_pairs={{0,2},{2,4},{4,6},{6,8},{8,10},{10,12},{12,14},{14,16},{16,18},{18... | collective-permute-start | bytes 3145736 | tf_op jit(solution)/shard_map/ppermute | solution.py:11
  156.3 18.6 %collective-permute-start.7 = (f32[1024,256]{1,0:T(8,128)S(1)}, f32[1024,256]{1,0:T(8,128)S(1)}, u32[]{:S(2)}, u32[]{:S(2)}) collective-permute-start(f32[1024,256]{1,0:T(8,128)S(1)} %bitcast_add_fusion), channel_id=1, source_target_pairs={{0,126},{2,0},{4,2},{6,4},{8,6},{10,8},{12,10},{14,12},{16,14},{18... | collective-permute-start | bytes 3145736 | tf_op jit(solution)/shard_map/ppermute | solution.py:11
  174.9 25.4 %copy-start.2 = (bf16[256,256]{1,0:T(8,128)(2,1)S(1)}, bf16[256,256]{1,0:T(8,128)(2,1)}, u32[]{:S(2)}) copy-start(bf16[256,256]{1,0:T(8,128)(2,1)} %param.8) | copy-start | bytes 393220
Sparse Core Ops, SparseCore 0:
  46.7 48.7 all-reduce.2
where the time goes:
time: 210 us; the launch traced here: 209 us
  waiting for transfers between devices  92.6 us (44%)
  local copies, waits for them, and re-layouts  25.8 us (12%)
  blocking collectives  25.2 us (12%)
  other arithmetic  22.9 us (11%)
  starting transfers between devices  16.4 us (8%)
  between operations  14.1 us (7%)
  matrix products  12.2 us (6%)
    psum x1, waiting for transfers between devices, shards(): preact = lax.psum(partial_value, 'rep') + bias  48.9 us
    ppermute x8, waiting for transfers between devices, passed_along(): lax.ppermute(array, axis, [(i, (i + by) % count) for i in range(count)])  43.7 us
    psum x1, blocking collectives, shards(): back_sum = lax.psum(gathered_sum, 'rep').astype(jnp.bfloat16)  25.2 us
    scatter-add x1, other arithmetic, backward_round(): jax.ops.segment_sum(products.reshape(-1, tile_size, feat_width), target.r...  19.2 us
    ppermute x8, starting transfers between devices, passed_along(): lax.ppermute(array, axis, [(i, (i + by) % count) for i in range(count)])  16.4 us
    reshape x1, local copies, waits for them, and re-layouts, backward_round(): products.reshape(-1, tile_size, feat_width)  9.01 us
    unnamed x14, local copies, waits for them, and re-layouts  5.47 us
    dot_general x1, matrix products, backward_round(): jnp.einsum('rsij,rif->rsjf', tile_values, scaled_tiles, preferred_element...  4.54 us
  transfers between devices with their start and end apart: 9, of which 7 were waited for; matrix products, arithmetic and copies ran while one was open for 3% of the time, Pallas kernels for 0%

commit v1 on v0

v1 whole, which is shorter than its diff:
```python
import jax
import jax.numpy as jnp
from jax import lax
from jax.sharding import PartitionSpec as P

REACH = 2


def passed_along(array, axis, by):
    count = lax.axis_size(axis)
    return lax.ppermute(array, axis, [(i, (i + by) % count) for i in range(count)])


def swapped(array, axis):
    count = lax.axis_size(axis)
    return lax.ppermute(array, axis, [(i, i ^ 1) for i in range(count)])


def silu_grad(preact):
    sigmoid_z = jax.nn.sigmoid(preact)
    return sigmoid_z * (1.0 + preact * (1.0 - sigmoid_z))


def activate(preact, mask_rows, cot_rows):
    output = jax.nn.silu(preact).astype(jnp.bfloat16)
    scaled = (
        mask_rows.astype(jnp.float32)[:, None] * cot_rows.astype(jnp.float32) * silu_grad(preact)
    ).astype(jnp.bfloat16)
    return (output, scaled)


def shards(features, weight, bias, cotangent, train_mask, tile_cols, tile_values):
    row_count, feat_width = features.shape
    tile_size = tile_values.shape[2]
    row_tiles = row_count // tile_size
    loop_size = lax.axis_size("blk")
    position = lax.axis_index("blk")
    span = 2 * REACH + 1
    window_count = span * row_tiles

    live_mask = tile_cols >= 0
    offset = jnp.mod(tile_cols // row_tiles - position + REACH, loop_size)
    local_index = jnp.where(live_mask, offset * row_tiles + tile_cols % row_tiles, -1)
    picks = (local_index[:, :, None] == jnp.arange(window_count)[None, None, :]).astype(jnp.bfloat16)
    dense = jnp.einsum(
        "rsw,rsij->riwj", picks, tile_values, preferred_element_type=jnp.float32
    ).astype(jnp.bfloat16)
    dense = dense.reshape(row_count, span, row_count)

    projected = jnp.dot(features, weight, preferred_element_type=jnp.float32).astype(jnp.bfloat16)
    slabs = []
    for k in range(span):
        shift = k - REACH
        slabs.append(projected if shift == 0 else passed_along(projected, "blk", -shift))

    partial_value = jnp.dot(dense[:, REACH], slabs[REACH], preferred_element_type=jnp.float32)
    for k in range(span):
        if k != REACH:
            partial_value = partial_value + jnp.dot(
                dense[:, k], slabs[k], preferred_element_type=jnp.float32
            )
    preact = (partial_value + swapped(partial_value, "rep")) + bias
    output, scaled = activate(preact, train_mask, cotangent)

    gathered_sum = jnp.dot(dense[:, REACH].T, scaled, preferred_element_type=jnp.float32)
    for k in range(span):
        shift = k - REACH
        if shift != 0:
            piece = jnp.dot(dense[:, k].T, scaled, preferred_element_type=jnp.float32)
            gathered_sum = gathered_sum + passed_along(piece, "blk", shift)
    back_sum = (gathered_sum + swapped(gathered_sum, "rep")).astype(jnp.bfloat16)
    grad_in = jnp.dot(back_sum, weight.T, preferred_element_type=jnp.float32).astype(jnp.bfloat16)
    return (output, grad_in)


def solution(mesh):
    placed = (
        P("blk", None),
        P(),
        P(),
        P("blk", None),
        P("blk"),
        P("blk", "rep"),
        P("blk", "rep", None, None),
    )
    return jax.shard_map(
        shards,
        mesh=mesh,
        in_specs=placed,
        out_specs=(P("blk", None), P("blk", None)),
        check_vma=False,
    )
```

time: 210 us -> 167 us (0.80)
  the two profiles are of different devices: /device:TPU:31 before, /device:TPU:1 now
where the time goes in v1:
time: 167 us; the launch traced here: 166 us
  waiting for transfers between devices  83.2 us (50%)
  local copies, waits for them, and re-layouts  39.2 us (23%)
  matrix products  21.7 us (13%)
  starting transfers between devices  19.3 us (12%)
  other arithmetic  2.04 us (1%)
    ppermute x2, waiting for transfers between devices, swapped(): return lax.ppermute(array, axis, [(i, i ^ 1) for i in range(count)])  43.7 us
    ppermute x8, waiting for transfers between devices, passed_along(): lax.ppermute(array, axis, [(i, (i + by) % count) for i in range(count)])  39.5 us
    convert_element_type x1, local copies, waits for them, and re-layouts, shards(): dense = jnp.einsum('rsw,rsij->riwj', picks, tile_values, preferred_elemen...  22.8 us
    reshape x1, local copies, waits for them, and re-layouts, shards(): dense = dense.reshape(row_count, span, row_count)  16.3 us
    ppermute x8, starting transfers between devices, passed_along(): lax.ppermute(array, axis, [(i, (i + by) % count) for i in range(count)])  12.3 us
    dot_general x4, matrix products, shards(): jnp.dot(dense[:, k], slabs[k], preferred_element_type=jnp.float32)  7.39 us
    ppermute x2, starting transfers between devices, swapped(): return lax.ppermute(array, axis, [(i, i ^ 1) for i in range(count)])  6.94 us
    dot_general x1, matrix products, shards(): jnp.einsum('rsw,rsij->riwj', picks, tile_values, preferred_element_type=j...  5.59 us
  transfers between devices with their start and end apart: 10, of which 5 were waited for; matrix products, arithmetic and copies ran while one was open for 33% of the time, Pallas kernels for 0%

profile of v1, /device:TPU:1, one launch (start us, length us, event | category | flops | bytes accessed | tf_op | source)
XLA Modules:
  0.0 166.2 jit_solution(7883690137776381203)
XLA Ops:
  0.6 0.0 copy-start
  0.6 1.5 convolution_convert_fusion.1
  2.2 2.2 %collective-permute-start = (bf16[1024,256]{1,0:T(8,128)(2,1)S(1)}, bf16[1024,256]{1,0:T(8,128)(2,1)}, u32[]{:S(2)}, u32[]{:S(2)}) collective-permute-start(bf16[1024,256]{1,0:T(8,128)(2,1)S(1)} %convolution_convert_fusion.1), channel_id=1, source_target_pairs={{0,4},{2,6},{4,8},{6,10},{8,12},{10,14},{12,16},{14,18},{16,20},{1... | collective-permute-start | bytes 1572872 | tf_op jit(solution)/shard_map/ppermute | solution.py:11
  4.3 5.1 %collective-permute-start.3 = (bf16[1024,256]{1,0:T(8,128)(2,1)S(1)}, bf16[1024,256]{1,0:T(8,128)(2,1)}, u32[]{:S(2)}, u32[]{:S(2)}) collective-permute-start(bf16[1024,256]{1,0:T(8,128)(2,1)S(1)} %convolution_convert_fusion.1), channel_id=1, source_target_pairs={{0,124},{2,126},{4,0},{6,2},{8,4},{10,6},{12,8},{14,10},{16,12},{1... | collective-permute-start | bytes 1572872 | tf_op jit(solution)/shard_map/ppermute | solution.py:11
  9.4 1.0 collective-permute-start.2
  10.4 0.8 collective-permute-start.1
  11.2 0.7 fusion.27
  11.9 0.0 copy-done
  11.9 5.6 %convert_bitcast_fusion = bf16[8,128,40,128]{3,2,1,0:T(8,128)(2,1)} fusion(bf16[8,8,128,128]{3,2,1,0:T(8,128)(2,1)S(1)} %copy-done, s32[8,8]{1,0:T(8,128)S(1)} %fusion.27), kind=kOutput, calls=%fused_computation | convolution fusion | flops 89131520 | bytes 12583168 | tf_op jit(solution)/shard_map/rsw,rsij->riwj/dot_general | solution.py:45
  17.5 22.8 %copy.11 = bf16[8,128,40,128]{1,0,3,2:T(8,128)(2,1)} copy(bf16[8,128,40,128]{3,2,1,0:T(8,128)(2,1)} %convert_bitcast_fusion) | data formatting | bytes 20971520 | tf_op jit(solution)/shard_map/convert_element_type | solution.py:47
  40.3 16.3 %reshape.10 = bf16[1024,5,1024]{0,2,1:T(8,128)(2,1)} reshape(bf16[8,128,40,128]{1,0,3,2:T(8,128)(2,1)} %copy.11) | data formatting | bytes 20971520 | tf_op jit(solution)/shard_map/reshape | solution.py:48
  56.6 2.5 %fusion.2 = f32[1024,256]{1,0:T(8,128)S(1)} fusion(bf16[1024,256]{1,0:T(8,128)(2,1)S(1)} %convolution_convert_fusion.1, bf16[1024,5,1024]{0,2,1:T(8,128)(2,1)} %reshape.10), kind=kOutput, calls=%fused_computation.8 | convolution fusion | flops 536870912 | bytes 3670016 | tf_op jit(solution)/shard_map/dot_general | solution.py:56
  59.1 0.0 collective-permute-done.3
  59.1 3.0 %fusion.10 = f32[1024,256]{1,0:T(8,128)S(1)} fusion(bf16[1024,256]{1,0:T(8,128)(2,1)} %collective-permute-done.3, bf16[1024,5,1024]{0,2,1:T(8,128)(2,1)} %reshape.10), kind=kOutput, calls=%fused_computation.16 | convolution fusion | flops 536870912 | bytes 3670016 | tf_op jit(solution)/shard_map/dot_general | solution.py:59
  62.1 0.0 copy-start.4
  62.1 0.0 copy-start.2
  62.1 0.0 copy-start.5
  62.1 0.0 collective-permute-done.2
  62.1 0.0 copy-done.1
  62.1 1.8 %fusion.8 = f32[1024,256]{1,0:T(8,128)S(1)} fusion(bf16[1024,256]{1,0:T(8,128)(2,1)} %collective-permute-done.2, bf16[1024,5,1024]{0,2,1:T(8,128)(2,1)S(1)} %copy-done.1), kind=kOutput, calls=%fused_computation.14 | convolution fusion | flops 536870912 | bytes 3670016 | tf_op jit(solution)/shard_map/dot_general | solution.py:59
  64.0 0.0 collective-permute-done
  64.0 1.8 %fusion.14 = f32[1024,256]{1,0:T(8,128)S(1)} fusion(f32[1024,256]{1,0:T(8,128)S(1)} %fusion.2, bf16[1024,256]{1,0:T(8,128)(2,1)} %collective-permute-done, bf16[1024,5,1024]{0,2,1:T(8,128)(2,1)S(1)} %copy-done.1), kind=kOutput, calls=%fused_computation.20 | convolution fusion | flops 537133056 | bytes 4718592 | tf_op jit(solution)/shard_map/dot_general | solution.py:59
  65.8 0.0 collective-permute-done.1
  65.8 0.8 fusion.13
  66.6 3.6 %collective-permute-start.4 = (f32[1024,256]{1,0:T(8,128)S(1)}, f32[1024,256]{1,0:T(8,128)S(1)}, u32[]{:S(2)}, u32[]{:S(2)}) collective-permute-start(f32[1024,256]{1,0:T(8,128)S(1)} %fusion.13), channel_id=1, source_target_pairs={{0,1},{1,0},{2,3},{3,2},{4,5},{5,4},{6,7},{7,6},{8,9},{9,8},{10,11... | collective-permute-start | bytes 3145736 | tf_op jit(solution)/shard_map/ppermute | solution.py:16
  70.2 0.0 copy-done.4
  70.2 23.5 %collective-permute-done.4 = f32[1024,256]{1,0:T(8,128)S(1)} collective-permute-done((f32[1024,256]{1,0:T(8,128)S(1)}, f32[1024,256]{1,0:T(8,128)S(1)}, u32[]{:S(2)}, u32[]{:S(2)}) %collective-permute-start.4) | collective-permute-done | bytes 1048608 | tf_op jit(solution)/shard_map/ppermute | solution.py:16
  93.6 0.0 copy-done.2
  93.6 0.0 copy-done.5
  93.6 1.3 multiply_convert_fusion
  95.0 0.7 fusion.3
  95.7 0.7 fusion.5
  96.4 0.0 copy-start.3
  96.4 0.7 fusion.7
  97.2 0.7 fusion.9
  97.9 1.5 collective-permute-start.5
  99.4 0.0 collective-permute-start.6
  99.4 1.7 %collective-permute-start.7 = (f32[1024,256]{1,0:T(8,128)S(1)}, f32[1024,256]{1,0:T(8,128)S(1)}, u32[]{:S(2)}, u32[]{:S(2)}) collective-permute-start(f32[1024,256]{1,0:T(8,128)S(1)} %fusion.7), channel_id=1, source_target_pairs={{0,2},{2,4},{4,6},{6,8},{8,10},{10,12},{12,14},{14,16},{16,18},{18... | collective-permute-start | bytes 3145736 | tf_op jit(solution)/shard_map/ppermute | solution.py:11
  101.1 0.1 collective-permute-start.8
  101.2 21.1 %collective-permute-done.5 = f32[1024,256]{1,0:T(8,128)S(1)} collective-permute-done((f32[1024,256]{1,0:T(8,128)S(1)}, f32[1024,256]{1,0:T(8,128)S(1)}, u32[]{:S(2)}, u32[]{:S(2)}) %collective-permute-start.5) | collective-permute-done | bytes 1048608 | tf_op jit(solution)/shard_map/ppermute | solution.py:11
  122.3 11.7 %collective-permute-done.6 = f32[1024,256]{1,0:T(8,128)S(1)} collective-permute-done((f32[1024,256]{1,0:T(8,128)S(1)}, f32[1024,256]{1,0:T(8,128)S(1)}, u32[]{:S(2)}, u32[]{:S(2)}) %collective-permute-start.6) | collective-permute-done | bytes 1048608 | tf_op jit(solution)/shard_map/ppermute | solution.py:11
  134.1 0.0 collective-permute-done.7
  134.1 6.6 %collective-permute-done.8 = f32[1024,256]{1,0:T(8,128)S(1)} collective-permute-done((f32[1024,256]{1,0:T(8,128)S(1)}, f32[1024,256]{1,0:T(8,128)S(1)}, u32[]{:S(2)}, u32[]{:S(2)}) %collective-permute-start.8) | collective-permute-done | bytes 1048608 | tf_op jit(solution)/shard_map/ppermute | solution.py:11
  140.7 0.7 fusion.18
  141.4 3.4 %collective-permute-start.9 = (f32[1024,256]{1,0:T(8,128)S(1)}, f32[1024,256]{1,0:T(8,128)S(1)}, u32[]{:S(2)}, u32[]{:S(2)}) collective-permute-start(f32[1024,256]{1,0:T(8,128)S(1)} %fusion.18), channel_id=1, source_target_pairs={{0,1},{1,0},{2,3},{3,2},{4,5},{5,4},{6,7},{7,6},{8,9},{9,8},{10,11... | collective-permute-start | bytes 3145736 | tf_op jit(solution)/shard_map/ppermute | solution.py:16
  144.8 20.2 %collective-permute-done.9 = f32[1024,256]{1,0:T(8,128)S(1)} collective-permute-done((f32[1024,256]{1,0:T(8,128)S(1)}, f32[1024,256]{1,0:T(8,128)S(1)}, u32[]{:S(2)}, u32[]{:S(2)}) %collective-permute-start.9) | collective-permute-done | bytes 1048608 | tf_op jit(solution)/shard_map/ppermute | solution.py:16
  165.0 0.0 copy-done.3
  165.0 1.2 convolution_convert_fusion
  (2 shorter events, 0.0 us)
Async XLA Ops:
  0.6 11.2 %copy-start = (bf16[8,8,128,128]{3,2,1,0:T(8,128)(2,1)S(1)}, bf16[8,8,128,128]{3,2,1,0:T(8,128)(2,1)}, u32[]{:S(2)}) copy-start(bf16[8,8,128,128]{3,2,1,0:T(8,128)(2,1)} %param.13) | copy-start | bytes 6291460
  2.2 61.8 %collective-permute-start = (bf16[1024,256]{1,0:T(8,128)(2,1)S(1)}, bf16[1024,256]{1,0:T(8,128)(2,1)}, u32[]{:S(2)}, u32[]{:S(2)}) collective-permute-start(bf16[1024,256]{1,0:T(8,128)(2,1)S(1)} %convolution_convert_fusion.1), channel_id=1, source_target_pairs={{0,4},{2,6},{4,8},{6,10},{8,12},{10,14},{12,16},{14,18},{16,20},{1... | collective-permute-start | bytes 1572872 | tf_op jit(solution)/shard_map/ppermute | solution.py:11
  4.3 54.7 %collective-permute-start.3 = (bf16[1024,256]{1,0:T(8,128)(2,1)S(1)}, bf16[1024,256]{1,0:T(8,128)(2,1)}, u32[]{:S(2)}, u32[]{:S(2)}) collective-permute-start(bf16[1024,256]{1,0:T(8,128)(2,1)S(1)} %convolution_convert_fusion.1), channel_id=1, source_target_pairs={{0,124},{2,126},{4,0},{6,2},{8,4},{10,6},{12,8},{14,10},{16,12},{1... | collective-permute-start | bytes 1572872 | tf_op jit(solution)/shard_map/ppermute | solution.py:11
  9.4 52.7 %collective-permute-start.2 = (bf16[1024,256]{1,0:T(8,128)(2,1)S(1)}, bf16[1024,256]{1,0:T(8,128)(2,1)}, u32[]{:S(2)}, u32[]{:S(2)}) collective-permute-start(bf16[1024,256]{1,0:T(8,128)(2,1)S(1)} %convolution_convert_fusion.1), channel_id=1, source_target_pairs={{0,126},{2,0},{4,2},{6,4},{8,6},{10,8},{12,10},{14,12},{16,14},{18... | collective-permute-start | bytes 1572872 | tf_op jit(solution)/shard_map/ppermute | solution.py:11
  10.4 55.4 %collective-permute-start.1 = (bf16[1024,256]{1,0:T(8,128)(2,1)S(1)}, bf16[1024,256]{1,0:T(8,128)(2,1)S(1)}, u32[]{:S(2)}, u32[]{:S(2)}) collective-permute-start(bf16[1024,256]{1,0:T(8,128)(2,1)S(1)} %convolution_convert_fusion.1), channel_id=1, source_target_pairs={{0,2},{2,4},{4,6},{6,8},{8,10},{10,12},{12,14},{14,16},{16,18},{18... | collective-permute-start | bytes 1572872 | tf_op jit(solution)/shard_map/ppermute | solution.py:11
  56.6 5.5 %copy-start.1 = (bf16[1024,5,1024]{0,2,1:T(8,128)(2,1)S(1)}, bf16[1024,5,1024]{0,2,1:T(8,128)(2,1)}, u32[]{:S(2)}) copy-start(bf16[1024,5,1024]{0,2,1:T(8,128)(2,1)} %reshape.10) | copy-start | bytes 31457284
  62.1 8.1 %copy-start.4 = (s32[1024]{0:T(1024)S(1)}, s32[1024]{0:T(1024)}, u32[]{:S(2)}) copy-start(s32[1024]{0:T(1024)} %param.11) | copy-start | bytes 12292
  62.1 31.6 %copy-start.2 = (bf16[1024,256]{1,0:T(8,128)(2,1)S(1)}, bf16[1024,256]{1,0:T(8,128)(2,1)}, u32[]{:S(2)}) copy-start(bf16[1024,256]{1,0:T(8,128)(2,1)} %param.10) | copy-start | bytes 1572868
  62.1 31.5 %copy-start.5 = (f32[256]{0:T(256)S(1)}, f32[256]{0:T(256)}, u32[]{:S(2)}) copy-start(f32[256]{0:T(256)} %param.9) | copy-start | bytes 3076
  66.6 27.0 %collective-permute-start.4 = (f32[1024,256]{1,0:T(8,128)S(1)}, f32[1024,256]{1,0:T(8,128)S(1)}, u32[]{:S(2)}, u32[]{:S(2)}) collective-permute-start(f32[1024,256]{1,0:T(8,128)S(1)} %fusion.13), channel_id=1, source_target_pairs={{0,1},{1,0},{2,3},{3,2},{4,5},{5,4},{6,7},{7,6},{8,9},{9,8},{10,11... | collective-permute-start | bytes 3145736 | tf_op jit(solution)/shard_map/ppermute | solution.py:16
  96.4 68.6 %copy-start.3 = (bf16[256,256]{1,0:T(8,128)(2,1)S(1)}, bf16[256,256]{1,0:T(8,128)(2,1)}, u32[]{:S(2)}) copy-start(bf16[256,256]{1,0:T(8,128)(2,1)} %param.8) | copy-start | bytes 393220
  97.9 24.4 %collective-permute-start.5 = (f32[1024,256]{1,0:T(8,128)S(1)}, f32[1024,256]{1,0:T(8,128)S(1)}, u32[]{:S(2)}, u32[]{:S(2)}) collective-permute-start(f32[1024,256]{1,0:T(8,128)S(1)} %fusion.3), channel_id=1, source_target_pairs={{0,124},{2,126},{4,0},{6,2},{8,4},{10,6},{12,8},{14,10},{16,12},{1... | collective-permute-start | bytes 3145736 | tf_op jit(solution)/shard_map/ppermute | solution.py:11
  99.4 34.7 %collective-permute-start.6 = (f32[1024,256]{1,0:T(8,128)S(1)}, f32[1024,256]{1,0:T(8,128)S(1)}, u32[]{:S(2)}, u32[]{:S(2)}) collective-permute-start(f32[1024,256]{1,0:T(8,128)S(1)} %fusion.5), channel_id=1, source_target_pairs={{0,126},{2,0},{4,2},{6,4},{8,6},{10,8},{12,10},{14,12},{16,14},{18... | collective-permute-start | bytes 3145736 | tf_op jit(solution)/shard_map/ppermute | solution.py:11
  99.4 34.7 %collective-permute-start.7 = (f32[1024,256]{1,0:T(8,128)S(1)}, f32[1024,256]{1,0:T(8,128)S(1)}, u32[]{:S(2)}, u32[]{:S(2)}) collective-permute-start(f32[1024,256]{1,0:T(8,128)S(1)} %fusion.7), channel_id=1, source_target_pairs={{0,2},{2,4},{4,6},{6,8},{8,10},{10,12},{12,14},{14,16},{16,18},{18... | collective-permute-start | bytes 3145736 | tf_op jit(solution)/shard_map/ppermute | solution.py:11
  101.1 39.6 %collective-permute-start.8 = (f32[1024,256]{1,0:T(8,128)S(1)}, f32[1024,256]{1,0:T(8,128)S(1)}, u32[]{:S(2)}, u32[]{:S(2)}) collective-permute-start(f32[1024,256]{1,0:T(8,128)S(1)} %fusion.9), channel_id=1, source_target_pairs={{0,4},{2,6},{4,8},{6,10},{8,12},{10,14},{12,16},{14,18},{16,20},{1... | collective-permute-start | bytes 3145736 | tf_op jit(solution)/shard_map/ppermute | solution.py:11
  141.4 23.6 %collective-permute-start.9 = (f32[1024,256]{1,0:T(8,128)S(1)}, f32[1024,256]{1,0:T(8,128)S(1)}, u32[]{:S(2)}, u32[]{:S(2)}) collective-permute-start(f32[1024,256]{1,0:T(8,128)S(1)} %fusion.18), channel_id=1, source_target_pairs={{0,1},{1,0},{2,3},{3,2},{4,5},{5,4},{6,7},{7,6},{8,9},{9,8},{10,11... | collective-permute-start | bytes 3145736 | tf_op jit(solution)/shard_map/ppermute | solution.py:16

commit v2 on v1

v2 whole, which is shorter than its diff:
```python
import jax
import jax.numpy as jnp
from jax import lax
from jax.experimental import pallas as pl
from jax.experimental.pallas import tpu as pltpu
from jax.sharding import PartitionSpec as P

REACH = 2


def passed_along(array, axis, by):
    count = lax.axis_size(axis)
    return lax.ppermute(array, axis, [(i, (i + by) % count) for i in range(count)])


def swapped(array, axis):
    count = lax.axis_size(axis)
    return lax.ppermute(array, axis, [(i, i ^ 1) for i in range(count)])


def silu_grad(preact):
    sigmoid_z = jax.nn.sigmoid(preact)
    return sigmoid_z * (1.0 + preact * (1.0 - sigmoid_z))


def activate(preact, mask_rows, cot_rows):
    output = jax.nn.silu(preact).astype(jnp.bfloat16)
    scaled = (
        mask_rows.astype(jnp.float32)[:, None] * cot_rows.astype(jnp.float32) * silu_grad(preact)
    ).astype(jnp.bfloat16)
    return (output, scaled)


def dense_block(local_index, tile_values, window_count):
    row_tiles, slots, tile_size, _ = tile_values.shape

    def kernel(index_ref, values_ref, out_ref):
        r = pl.program_id(0)
        out_ref[...] = jnp.zeros_like(out_ref)
        for s in range(slots):
            w = index_ref[r, s]

            @pl.when((w >= 0) & (w < window_count))
            def _():
                start = pl.multiple_of(w * tile_size, tile_size)
                out_ref[:, pl.ds(start, tile_size)] = values_ref[0, s]

    return pl.pallas_call(
        kernel,
        grid_spec=pltpu.PrefetchScalarGridSpec(
            num_scalar_prefetch=1,
            grid=(row_tiles,),
            in_specs=[pl.BlockSpec((1, slots, tile_size, tile_size), lambda r, idx: (r, 0, 0, 0))],
            out_specs=pl.BlockSpec((tile_size, window_count * tile_size), lambda r, idx: (r, 0)),
        ),
        out_shape=jax.ShapeDtypeStruct((row_tiles * tile_size, window_count * tile_size), tile_values.dtype),
    )(local_index, tile_values)


def shards(features, weight, bias, cotangent, train_mask, tile_cols, tile_values):
    row_count, feat_width = features.shape
    tile_size = tile_values.shape[2]
    row_tiles = row_count // tile_size
    loop_size = lax.axis_size("blk")
    position = lax.axis_index("blk")
    span = 2 * REACH + 1
    window_count = span * row_tiles

    live_mask = tile_cols >= 0
    offset = jnp.mod(tile_cols // row_tiles - position + REACH, loop_size)
    local_index = jnp.where(live_mask, offset * row_tiles + tile_cols % row_tiles, -1)
    dense = dense_block(local_index, tile_values, window_count)
    blocks = [dense[:, k * row_count:(k + 1) * row_count] for k in range(span)]

    projected = jnp.dot(features, weight, preferred_element_type=jnp.float32).astype(jnp.bfloat16)
    slabs = []
    for k in range(span):
        shift = k - REACH
        slabs.append(projected if shift == 0 else passed_along(projected, "blk", -shift))

    partial_value = jnp.dot(blocks[REACH], slabs[REACH], preferred_element_type=jnp.float32)
    for k in range(span):
        if k != REACH:
            partial_value = partial_value + jnp.dot(blocks[k], slabs[k], preferred_element_type=jnp.float32)
    partial_value = partial_value.astype(jnp.bfloat16)
    preact = (
        partial_value.astype(jnp.float32) + swapped(partial_value, "rep").astype(jnp.float32)
    ) + bias
    output, scaled = activate(preact, train_mask, cotangent)

    contract_rows = (((0,), (0,)), ((), ()))
    gathered_sum = lax.dot_general(
        scaled, blocks[REACH], contract_rows, preferred_element_type=jnp.float32
    )
    for k in range(span):
        shift = k - REACH
        if shift != 0:
            piece = lax.dot_general(scaled, blocks[k], contract_rows, preferred_element_type=jnp.float32)
            gathered_sum = gathered_sum + passed_along(piece.astype(jnp.bfloat16), "blk", shift).astype(
                jnp.float32
            )
    gathered_sum = gathered_sum.astype(jnp.bfloat16)
    back_sum_t = (
        gathered_sum.astype(jnp.float32) + swapped(gathered_sum, "rep").astype(jnp.float32)
    ).astype(jnp.bfloat16)
    grad_in = lax.dot_general(
        back_sum_t, weight, (((0,), (1,)), ((), ())), preferred_element_type=jnp.float32
    ).astype(jnp.bfloat16)
    return (output, grad_in)


def solution(mesh):
    placed = (
        P("blk", None),
        P(),
        P(),
        P("blk", None),
        P("blk"),
        P("blk", "rep"),
        P("blk", "rep", None, None),
    )
    return jax.shard_map(
        shards,
        mesh=mesh,
        in_specs=placed,
        out_specs=(P("blk", None), P("blk", None)),
        check_vma=False,
    )
```

time: 167 us -> 93.2 us (0.56)
  local copies, waits for them, and re-layouts: 39.2 us -> 1.07 us
  waiting for transfers between devices: 83.2 us -> 45.9 us
  matrix products: 21.7 us -> 13.5 us
  Pallas kernels: 0 us -> 8.15 us
    ppermute x2, waiting for transfers between devices: 43.7 us -> 18.2 us  [swapped(): return lax.ppermute(array, axis, [(i, i ^ 1) for i in range(count)])]
    convert_element_type x1 -> x0, local copies, waits for them, and re-layouts: 22.8 us -> none  [shards(): dense = jnp.einsum('rsw,rsij->riwj', picks, tile_values, preferred_elemen...]
    reshape x1 -> x0, local copies, waits for them, and re-layouts: 16.3 us -> none  [shards(): dense = dense.reshape(row_count, span, row_count)]
    ppermute x8, waiting for transfers between devices: 39.5 us -> 27.7 us  [passed_along(): lax.ppermute(array, axis, [(i, (i + by) % count) for i in range(count)])]
    pallas_call x0 -> x1, Pallas kernels: none -> 8.15 us  [dense_block(): pl.pallas_call(kernel, grid_spec=pltpu.PrefetchScalarGridSpec(num_scalar_...]
    dot_general x12 -> x11, matrix products: 20.2 us -> 12.3 us  [the longest x4 4.99 us: shards(): jnp.dot(blocks[k], slabs[k], preferred_element_type=jnp.float32)]
  transfers between devices with their start and end apart: 10 -> 10, of which waited for: 5 -> 6; matrix products, arithmetic and copies ran while one was open for 33% -> 9% of each run, Pallas kernels for 0% -> 9%
where the time goes in v2:
time: 93.2 us; the launch traced here: 92.8 us
  waiting for transfers between devices  45.9 us (49%)
  starting transfers between devices  20.3 us (22%)
  matrix products  13.5 us (14%)
  Pallas kernels  8.15 us (9%)
  other arithmetic  3.16 us (3%)
  local copies, waits for them, and re-layouts  1.07 us (1%)
    ppermute x8, waiting for transfers between devices, passed_along(): lax.ppermute(array, axis, [(i, (i + by) % count) for i in range(count)])  27.7 us
    ppermute x2, waiting for transfers between devices, swapped(): return lax.ppermute(array, axis, [(i, i ^ 1) for i in range(count)])  18.2 us
    ppermute x8, starting transfers between devices, passed_along(): lax.ppermute(array, axis, [(i, (i + by) % count) for i in range(count)])  13.3 us
    pallas_call x1, Pallas kernels, dense_block(): pl.pallas_call(kernel, grid_spec=pltpu.PrefetchScalarGridSpec(num_scalar_...  8.15 us
    ppermute x2, starting transfers between devices, swapped(): return lax.ppermute(array, axis, [(i, i ^ 1) for i in range(count)])  6.95 us
    dot_general x4, matrix products, shards(): jnp.dot(blocks[k], slabs[k], preferred_element_type=jnp.float32)  4.99 us
    dot_general x4, matrix products, shards(): lax.dot_general(scaled, blocks[k], contract_rows, preferred_element_type=...  2.93 us
    dot_general x1, matrix products, shards(): jnp.dot(blocks[REACH], slabs[REACH], preferred_element_type=jnp.float32)  2.45 us
  transfers between devices with their start and end apart: 10, of which 6 were waited for; matrix products, arithmetic and copies ran while one was open for 9% of the time, Pallas kernels for 9%

profile of v2, /device:TPU:1, one launch (start us, length us, event | category | flops | bytes accessed | tf_op | source)
XLA Modules:
  0.0 92.8 jit_solution(6297376243238799038)
XLA Ops:
  0.6 0.0 copy-start
  0.6 1.0 %copy-done = bf16[1024,256]{1,0:T(8,128)(2,1)S(1)} copy-done((bf16[1024,256]{1,0:T(8,128)(2,1)S(1)}, bf16[1024,256]{1,0:T(8,128)(2,1)}, u32[]{:S(2)}) %copy-start) | copy-done | bytes 524312
  1.7 1.2 %convolution_convert_fusion.1 = bf16[1024,256]{1,0:T(8,128)(2,1)S(1)} fusion(bf16[1024,256]{1,0:T(8,128)(2,1)S(1)} %copy-done, bf16[256,256]{1,0:T(8,128)(2,1)} %param.8), kind=kOutput, calls=%fused_computation.26 | convolution fusion | flops 134479872 | bytes 1179648 | tf_op jit(solution)/shard_map/dot_general | solution.py:75
  2.9 7.2 %collective-permute-start.3 = (bf16[1024,256]{1,0:T(8,128)(2,1)S(1)}, bf16[1024,256]{1,0:T(8,128)(2,1)S(1)}, u32[]{:S(2)}, u32[]{:S(2)}) collective-permute-start(bf16[1024,256]{1,0:T(8,128)(2,1)S(1)} %convolution_convert_fusion.1), channel_id=1, source_target_pairs={{0,124},{2,126},{4,0},{6,2},{8,4},{10,6},{12,8},{14,10},{16,12},{1... | collective-permute-start | bytes 1572872 | tf_op jit(solution)/shard_map/ppermute | solution.py:13
  10.1 1.0 %collective-permute-start.2 = (bf16[1024,256]{1,0:T(8,128)(2,1)S(1)}, bf16[1024,256]{1,0:T(8,128)(2,1)S(1)}, u32[]{:S(2)}, u32[]{:S(2)}) collective-permute-start(bf16[1024,256]{1,0:T(8,128)(2,1)S(1)} %convolution_convert_fusion.1), channel_id=1, source_target_pairs={{0,126},{2,0},{4,2},{6,4},{8,6},{10,8},{12,10},{14,12},{16,14},{18... | collective-permute-start | bytes 1572872 | tf_op jit(solution)/shard_map/ppermute | solution.py:13
  11.0 0.8 collective-permute-start.1
  11.8 0.0 collective-permute-start
  11.8 1.3 %fusion.52.index_ref = s32[8,8]{1,0:T(8,128)} fusion(s32[8,8]{1,0:T(8,128)} %param.12, s32[]{:T(128)S(6)} %axis_index.15), kind=kLoop, calls=%fused_computation.50 | loop fusion | flops 2304 | bytes 516 | tf_op jit(solution)/shard_map/jit(_where)/select_n | solution.py:71
  13.1 8.2 %shard_map.86 = bf16[1024,5120]{1,0:T(8,128)(2,1)} custom-call(s32[8,8]{1,0:T(8,128)} %fusion.52.index_ref, bf16[8,8,128,128]{3,2,1,0:T(8,128)(2,1)} %values_ref.1), custom_call_target="tpu_custom_call" | custom-call | tf_op jit(solution)/shard_map/pallas_call | solution.py:48
  21.3 0.0 copy-start.1
  21.3 2.5 %fusion.18 = f32[1024,256]{1,0:T(8,128)S(1)} fusion(bf16[1024,256]{1,0:T(8,128)(2,1)S(1)} %convolution_convert_fusion.1, bf16[1024,5120]{1,0:T(8,128)(2,1)} %shard_map.86), kind=kOutput, calls=%fused_computation.18 | convolution fusion | flops 536870912 | bytes 3670016 | tf_op jit(solution)/shard_map/dot_general | solution.py:81
  23.7 0.0 collective-permute-done.3
  23.7 2.8 %fusion.2 = f32[1024,256]{1,0:T(8,128)S(1)} fusion(bf16[1024,256]{1,0:T(8,128)(2,1)S(1)} %collective-permute-done.3, bf16[1024,5120]{1,0:T(8,128)(2,1)} %shard_map.86), kind=kOutput, calls=%fused_computation.2 | convolution fusion | flops 536870912 | bytes 3670016 | tf_op jit(solution)/shard_map/dot_general | solution.py:84
  26.6 0.0 copy-start.4
  26.6 0.0 copy-start.2
  26.6 0.0 copy-start.5
  26.6 0.0 collective-permute-done.2
  26.6 0.0 copy-done.1
  26.6 0.7 fusion.6
  27.4 0.0 collective-permute-done.1
  27.4 0.7 fusion.10
  28.1 6.3 %collective-permute-done = bf16[1024,256]{1,0:T(8,128)(2,1)S(1)} collective-permute-done((bf16[1024,256]{1,0:T(8,128)(2,1)S(1)}, bf16[1024,256]{1,0:T(8,128)(2,1)S(1)}, u32[]{:S(2)}, u32[]{:S(2)}) %collective-permute-start) | collective-permute-done | bytes 524320 | tf_op jit(solution)/shard_map/ppermute | solution.py:13
  34.4 0.7 fusion.32
  35.1 3.5 %collective-permute-start.4 = (bf16[1024,256]{1,0:T(8,128)(2,1)S(1)}, bf16[1024,256]{1,0:T(8,128)(2,1)S(1)}, u32[]{:S(2)}, u32[]{:S(2)}) collective-permute-start(bf16[1024,256]{1,0:T(8,128)(2,1)S(1)} %fusion.32), channel_id=1, source_target_pairs={{0,1},{1,0},{2,3},{3,2},{4,5},{5,4},{6,7},{7,6},{8,9},{9,8},{10,11... | collective-permute-start | bytes 1572872 | tf_op jit(solution)/shard_map/ppermute | solution.py:18
  38.6 0.0 copy-done.4
  38.6 9.0 %collective-permute-done.4 = bf16[1024,256]{1,0:T(8,128)(2,1)S(1)} collective-permute-done((bf16[1024,256]{1,0:T(8,128)(2,1)S(1)}, bf16[1024,256]{1,0:T(8,128)(2,1)S(1)}, u32[]{:S(2)}, u32[]{:S(2)}) %collective-permute-start.4) | collective-permute-done | bytes 524320 | tf_op jit(solution)/shard_map/ppermute | solution.py:18
  47.6 0.0 copy-done.2
  47.6 0.0 copy-done.5
  47.6 1.4 %multiply_convert_fusion = (bf16[1024,256]{1,0:T(8,128)(2,1)S(1)}, bf16[1024,256]{1,0:T(8,128)(2,1)}) fusion(bf16[1024,256]{1,0:T(8,128)(2,1)S(1)} %copy-done.2, bf16[1024,256]{1,0:T(8,128)(2,1)S(1)} %collective-permute-done.4, bf16[1024,256]{1,0:T(8,128)(2,1)S(1)} %fusion.32, f32[1024]{0:T(1024)S(1)} %convert_element_type.68, f32[256]{0:T(256)S(1)} %copy-done.5), kind=kLoop, calls=%fused_computation.33 | loop fusion | flops 4456448 | bytes 2626560 | tf_op jit(solution)/shard_map/convert_element_type | solution.py:30
  49.0 0.0 copy-start.3
  49.0 0.7 fusion.44
  49.7 0.7 fusion.41
  50.5 0.7 fusion.38
  51.2 0.7 fusion.35
  51.9 2.7 %collective-permute-start.5 = (bf16[256,1024]{1,0:T(8,128)(2,1)S(1)}, bf16[256,1024]{1,0:T(8,128)(2,1)S(1)}, u32[]{:S(2)}, u32[]{:S(2)}) collective-permute-start(bf16[256,1024]{1,0:T(8,128)(2,1)S(1)} %fusion.35), channel_id=1, source_target_pairs={{0,124},{2,126},{4,0},{6,2},{8,4},{10,6},{12,8},{14,10},{16,12},{1... | collective-permute-start | bytes 1572872 | tf_op jit(solution)/shard_map/ppermute | solution.py:13
  54.6 0.2 collective-permute-start.6
  54.8 1.5 %collective-permute-start.7 = (bf16[256,1024]{1,0:T(8,128)(2,1)S(1)}, bf16[256,1024]{1,0:T(8,128)(2,1)S(1)}, u32[]{:S(2)}, u32[]{:S(2)}) collective-permute-start(bf16[256,1024]{1,0:T(8,128)(2,1)S(1)} %fusion.41), channel_id=1, source_target_pairs={{0,2},{2,4},{4,6},{6,8},{8,10},{10,12},{12,14},{14,16},{16,18},{18... | collective-permute-start | bytes 1572872 | tf_op jit(solution)/shard_map/ppermute | solution.py:13
  56.4 0.0 collective-permute-start.8
  56.4 0.7 fusion.16
  57.1 8.9 %collective-permute-done.5 = bf16[256,1024]{1,0:T(8,128)(2,1)S(1)} collective-permute-done((bf16[256,1024]{1,0:T(8,128)(2,1)S(1)}, bf16[256,1024]{1,0:T(8,128)(2,1)S(1)}, u32[]{:S(2)}, u32[]{:S(2)}) %collective-permute-start.5) | collective-permute-done | bytes 524320 | tf_op jit(solution)/shard_map/ppermute | solution.py:13
  66.0 3.4 %collective-permute-done.6 = bf16[256,1024]{1,0:T(8,128)(2,1)S(1)} collective-permute-done((bf16[256,1024]{1,0:T(8,128)(2,1)S(1)}, bf16[256,1024]{1,0:T(8,128)(2,1)S(1)}, u32[]{:S(2)}, u32[]{:S(2)}) %collective-permute-start.6) | collective-permute-done | bytes 524320 | tf_op jit(solution)/shard_map/ppermute | solution.py:13
  69.5 0.0 collective-permute-done.7
  69.5 9.0 %collective-permute-done.8 = bf16[256,1024]{1,0:T(8,128)(2,1)S(1)} collective-permute-done((bf16[256,1024]{1,0:T(8,128)(2,1)S(1)}, bf16[256,1024]{1,0:T(8,128)(2,1)S(1)}, u32[]{:S(2)}, u32[]{:S(2)}) %collective-permute-start.8) | collective-permute-done | bytes 524320 | tf_op jit(solution)/shard_map/ppermute | solution.py:13
  78.5 0.5 add_convert_fusion.1
  78.9 3.5 %collective-permute-start.9 = (bf16[256,1024]{1,0:T(8,128)(2,1)S(1)}, bf16[256,1024]{1,0:T(8,128)(2,1)S(1)}, u32[]{:S(2)}, u32[]{:S(2)}) collective-permute-start(bf16[256,1024]{1,0:T(8,128)(2,1)S(1)} %add_convert_fusion.1), channel_id=1, source_target_pairs={{0,1},{1,0},{2,3},{3,2},{4,5},{5,4},{6,7},{7,6},{8,9},{9,8},{10,11... | collective-permute-start | bytes 1572872 | tf_op jit(solution)/shard_map/ppermute | solution.py:18
  82.4 9.2 %collective-permute-done.9 = bf16[256,1024]{1,0:T(8,128)(2,1)S(1)} collective-permute-done((bf16[256,1024]{1,0:T(8,128)(2,1)S(1)}, bf16[256,1024]{1,0:T(8,128)(2,1)S(1)}, u32[]{:S(2)}, u32[]{:S(2)}) %collective-permute-start.9) | collective-permute-done | bytes 524320 | tf_op jit(solution)/shard_map/ppermute | solution.py:18
  91.6 0.0 copy-done.3
  91.6 1.2 %convolution_convert_fusion = bf16[1024,256]{1,0:T(8,128)(2,1)} fusion(bf16[256,256]{1,0:T(8,128)(2,1)S(1)} %copy-done.3, bf16[256,1024]{1,0:T(8,128)(2,1)S(1)} %collective-permute-done.9, bf16[256,1024]{1,0:T(8,128)(2,1)S(1)} %add_convert_fusion.1), kind=kOutput, calls=%fused_computation.25 | convolution fusion | flops 135528448 | bytes 1703936 | tf_op jit(solution)/shard_map/dot_general | solution.py:106
  (1 shorter events, 0.0 us)
Async XLA Ops:
  0.6 1.0 %copy-start = (bf16[1024,256]{1,0:T(8,128)(2,1)S(1)}, bf16[1024,256]{1,0:T(8,128)(2,1)}, u32[]{:S(2)}) copy-start(bf16[1024,256]{1,0:T(8,128)(2,1)} %param.7) | copy-start | bytes 1572868
  2.9 20.8 %collective-permute-start.3 = (bf16[1024,256]{1,0:T(8,128)(2,1)S(1)}, bf16[1024,256]{1,0:T(8,128)(2,1)S(1)}, u32[]{:S(2)}, u32[]{:S(2)}) collective-permute-start(bf16[1024,256]{1,0:T(8,128)(2,1)S(1)} %convolution_convert_fusion.1), channel_id=1, source_target_pairs={{0,124},{2,126},{4,0},{6,2},{8,4},{10,6},{12,8},{14,10},{16,12},{1... | collective-permute-start | bytes 1572872 | tf_op jit(solution)/shard_map/ppermute | solution.py:13
  10.1 16.6 %collective-permute-start.2 = (bf16[1024,256]{1,0:T(8,128)(2,1)S(1)}, bf16[1024,256]{1,0:T(8,128)(2,1)S(1)}, u32[]{:S(2)}, u32[]{:S(2)}) collective-permute-start(bf16[1024,256]{1,0:T(8,128)(2,1)S(1)} %convolution_convert_fusion.1), channel_id=1, source_target_pairs={{0,126},{2,0},{4,2},{6,4},{8,6},{10,8},{12,10},{14,12},{16,14},{18... | collective-permute-start | bytes 1572872 | tf_op jit(solution)/shard_map/ppermute | solution.py:13
  11.0 16.4 %collective-permute-start.1 = (bf16[1024,256]{1,0:T(8,128)(2,1)S(1)}, bf16[1024,256]{1,0:T(8,128)(2,1)S(1)}, u32[]{:S(2)}, u32[]{:S(2)}) collective-permute-start(bf16[1024,256]{1,0:T(8,128)(2,1)S(1)} %convolution_convert_fusion.1), channel_id=1, source_target_pairs={{0,2},{2,4},{4,6},{6,8},{8,10},{10,12},{12,14},{14,16},{16,18},{18... | collective-permute-start | bytes 1572872 | tf_op jit(solution)/shard_map/ppermute | solution.py:13
  11.8 22.6 %collective-permute-start = (bf16[1024,256]{1,0:T(8,128)(2,1)S(1)}, bf16[1024,256]{1,0:T(8,128)(2,1)S(1)}, u32[]{:S(2)}, u32[]{:S(2)}) collective-permute-start(bf16[1024,256]{1,0:T(8,128)(2,1)S(1)} %convolution_convert_fusion.1), channel_id=1, source_target_pairs={{0,4},{2,6},{4,8},{6,10},{8,12},{10,14},{12,16},{14,18},{16,20},{1... | collective-permute-start | bytes 1572872 | tf_op jit(solution)/shard_map/ppermute | solution.py:13
  21.3 5.4 %copy-start.1 = (bf16[1024,5120]{1,0:T(8,128)(2,1)S(1)}, bf16[1024,5120]{1,0:T(8,128)(2,1)}, u32[]{:S(2)}) copy-start(bf16[1024,5120]{1,0:T(8,128)(2,1)} %shard_map.86) | copy-start | bytes 31457284
  26.6 12.0 %copy-start.4 = (s32[1024]{0:T(1024)S(1)}, s32[1024]{0:T(1024)}, u32[]{:S(2)}) copy-start(s32[1024]{0:T(1024)} %param.11) | copy-start | bytes 12292
  26.6 21.0 %copy-start.2 = (bf16[1024,256]{1,0:T(8,128)(2,1)S(1)}, bf16[1024,256]{1,0:T(8,128)(2,1)}, u32[]{:S(2)}) copy-start(bf16[1024,256]{1,0:T(8,128)(2,1)} %param.10) | copy-start | bytes 1572868
  26.6 21.0 %copy-start.5 = (f32[256]{0:T(256)S(1)}, f32[256]{0:T(256)}, u32[]{:S(2)}) copy-start(f32[256]{0:T(256)} %param.9) | copy-start | bytes 3076
  35.1 12.5 %collective-permute-start.4 = (bf16[1024,256]{1,0:T(8,128)(2,1)S(1)}, bf16[1024,256]{1,0:T(8,128)(2,1)S(1)}, u32[]{:S(2)}, u32[]{:S(2)}) collective-permute-start(bf16[1024,256]{1,0:T(8,128)(2,1)S(1)} %fusion.32), channel_id=1, source_target_pairs={{0,1},{1,0},{2,3},{3,2},{4,5},{5,4},{6,7},{7,6},{8,9},{9,8},{10,11... | collective-permute-start | bytes 1572872 | tf_op jit(solution)/shard_map/ppermute | solution.py:18
  49.0 42.7 %copy-start.3 = (bf16[256,256]{1,0:T(8,128)(2,1)S(1)}, bf16[256,256]{1,0:T(8,128)(2,1)}, u32[]{:S(2)}) copy-start(bf16[256,256]{1,0:T(8,128)(2,1)} %param.8) | copy-start | bytes 393220
  51.9 14.1 %collective-permute-start.5 = (bf16[256,1024]{1,0:T(8,128)(2,1)S(1)}, bf16[256,1024]{1,0:T(8,128)(2,1)S(1)}, u32[]{:S(2)}, u32[]{:S(2)}) collective-permute-start(bf16[256,1024]{1,0:T(8,128)(2,1)S(1)} %fusion.35), channel_id=1, source_target_pairs={{0,124},{2,126},{4,0},{6,2},{8,4},{10,6},{12,8},{14,10},{16,12},{1... | collective-permute-start | bytes 1572872 | tf_op jit(solution)/shard_map/ppermute | solution.py:13
  54.6 14.8 %collective-permute-start.6 = (bf16[256,1024]{1,0:T(8,128)(2,1)S(1)}, bf16[256,1024]{1,0:T(8,128)(2,1)S(1)}, u32[]{:S(2)}, u32[]{:S(2)}) collective-permute-start(bf16[256,1024]{1,0:T(8,128)(2,1)S(1)} %fusion.38), channel_id=1, source_target_pairs={{0,126},{2,0},{4,2},{6,4},{8,6},{10,8},{12,10},{14,12},{16,14},{18... | collective-permute-start | bytes 1572872 | tf_op jit(solution)/shard_map/ppermute | solution.py:13
  54.8 14.6 %collective-permute-start.7 = (bf16[256,1024]{1,0:T(8,128)(2,1)S(1)}, bf16[256,1024]{1,0:T(8,128)(2,1)S(1)}, u32[]{:S(2)}, u32[]{:S(2)}) collective-permute-start(bf16[256,1024]{1,0:T(8,128)(2,1)S(1)} %fusion.41), channel_id=1, source_target_pairs={{0,2},{2,4},{4,6},{6,8},{8,10},{10,12},{12,14},{14,16},{16,18},{18... | collective-permute-start | bytes 1572872 | tf_op jit(solution)/shard_map/ppermute | solution.py:13
  56.4 22.1 %collective-permute-start.8 = (bf16[256,1024]{1,0:T(8,128)(2,1)S(1)}, bf16[256,1024]{1,0:T(8,128)(2,1)S(1)}, u32[]{:S(2)}, u32[]{:S(2)}) collective-permute-start(bf16[256,1024]{1,0:T(8,128)(2,1)S(1)} %fusion.44), channel_id=1, source_target_pairs={{0,4},{2,6},{4,8},{6,10},{8,12},{10,14},{12,16},{14,18},{16,20},{1... | collective-permute-start | bytes 1572872 | tf_op jit(solution)/shard_map/ppermute | solution.py:13
  78.9 12.7 %collective-permute-start.9 = (bf16[256,1024]{1,0:T(8,128)(2,1)S(1)}, bf16[256,1024]{1,0:T(8,128)(2,1)S(1)}, u32[]{:S(2)}, u32[]{:S(2)}) collective-permute-start(bf16[256,1024]{1,0:T(8,128)(2,1)S(1)} %add_convert_fusion.1), channel_id=1, source_target_pairs={{0,1},{1,0},{2,3},{3,2},{4,5},{5,4},{6,7},{7,6},{8,9},{9,8},{10,11... | collective-permute-start | bytes 1572872 | tf_op jit(solution)/shard_map/ppermute | solution.py:18

commit v3 on v2

--- a/solution.py
+++ b/solution.py
@@ -31,46 +31,52 @@
     return (output, scaled)
 
 
-def dense_block(local_index, tile_values, window_count):
-    row_tiles, slots, tile_size, _ = tile_values.shape
+def dense_block(local_index, own_values, other_values, window_count):
+    row_tiles, slots, tile_size, _ = own_values.shape
 
-    def kernel(index_ref, values_ref, out_ref):
+    def kernel(index_ref, own_ref, other_ref, out_ref):
         r = pl.program_id(0)
         out_ref[...] = jnp.zeros_like(out_ref)
-        for s in range(slots):
-            w = index_ref[r, s]
+        for half, values_ref in enumerate((own_ref, other_ref)):
+            for s in range(slots):
+                w = index_ref[r, half * slots + s]
 
-            @pl.when((w >= 0) & (w < window_count))
-            def _():
-                start = pl.multiple_of(w * tile_size, tile_size)
-                out_ref[:, pl.ds(start, tile_size)] = values_ref[0, s]
+                @pl.when((w >= 0) & (w < window_count))
+                def _():
+                    start = pl.multiple_of(w * tile_size, tile_size)
+                    out_ref[:, pl.ds(start, tile_size)] = values_ref[0, s]
 
+    tile_spec = pl.BlockSpec((1, slots, tile_size, tile_size), lambda r, idx: (r, 0, 0, 0))
     return pl.pallas_call(
         kernel,
         grid_spec=pltpu.PrefetchScalarGridSpec(
             num_scalar_prefetch=1,
             grid=(row_tiles,),
-            in_specs=[pl.BlockSpec((1, slots, tile_size, tile_size), lambda r, idx: (r, 0, 0, 0))],
+            in_specs=[tile_spec, tile_spec],
             out_specs=pl.BlockSpec((tile_size, window_count * tile_size), lambda r, idx: (r, 0)),
         ),
-        out_shape=jax.ShapeDtypeStruct((row_tiles * tile_size, window_count * tile_size), tile_values.dtype),
-    )(local_index, tile_values)
+        out_shape=jax.ShapeDtypeStruct((row_tiles * tile_size, window_count * tile_size), own_values.dtype),
+    )(local_index, own_values, other_values)
 
 
 def shards(features, weight, bias, cotangent, train_mask, tile_cols, tile_values):
     row_count, feat_width = features.shape
     tile_size = tile_values.shape[2]
     row_tiles = row_count // tile_size
+    half_tiles = row_tiles // 2
+    half_rows = row_count // 2
     loop_size = lax.axis_size("blk")
     position = lax.axis_index("blk")
+    side = lax.axis_index("rep")
     span = 2 * REACH + 1
     window_count = span * row_tiles
 
-    live_mask = tile_cols >= 0
-    offset = jnp.mod(tile_cols // row_tiles - position + REACH, loop_size)
-    local_index = jnp.where(live_mask, offset * row_tiles + tile_cols % row_tiles, -1)
-    dense = dense_block(local_index, tile_values, window_count)
-    blocks = [dense[:, k * row_count:(k + 1) * row_count] for k in range(span)]
+    tile_values = tile_values.reshape((2, half_tiles) + tile_values.shape[1:])
+    tile_cols = tile_cols.reshape((2, half_tiles) + tile_cols.shape[1:])
+    own_values = tile_values[side]
+    other_values = swapped(tile_values[1 - side], "rep")
+    own_cols = tile_cols[side]
+    other_cols = swapped(tile_cols[1 - side], "rep")
 
     projected = jnp.dot(features, weight, preferred_element_type=jnp.float32).astype(jnp.bfloat16)
     slabs = []
@@ -78,15 +84,25 @@
         shift = k - REACH
         slabs.append(projected if shift == 0 else passed_along(projected, "blk", -shift))
 
+    cols = jnp.concatenate([own_cols, other_cols], axis=1)
+    live_mask = cols >= 0
+    offset = jnp.mod(cols // row_tiles - position + REACH, loop_size)
+    local_index = jnp.where(live_mask, offset * row_tiles + cols % row_tiles, -1)
+    dense = dense_block(local_index, own_values, other_values, window_count)
+    blocks = [dense[:, k * row_count:(k + 1) * row_count] for k in range(span)]
+
     partial_value = jnp.dot(blocks[REACH], slabs[REACH], preferred_element_type=jnp.float32)
     for k in range(span):
         if k != REACH:
             partial_value = partial_value + jnp.dot(blocks[k], slabs[k], preferred_element_type=jnp.float32)
-    partial_value = partial_value.astype(jnp.bfloat16)
-    preact = (
-        partial_value.astype(jnp.float32) + swapped(partial_value, "rep").astype(jnp.float32)
-    ) + bias
-    output, scaled = activate(preact, train_mask, cotangent)
+    preact = partial_value + bias
+    mask_rows = lax.dynamic_slice_in_dim(train_mask, side * half_rows, half_rows)
+    cot_rows = lax.dynamic_slice_in_dim(cotangent, side * half_rows, half_rows)
+    own_output, scaled = activate(preact, mask_rows, cot_rows)
+    other_output = swapped(own_output, "rep")
+    output = jnp.concatenate(
+        [jnp.where(side == 0, own_output, other_output), jnp.where(side == 0, other_output, own_output)], axis=0
+    )
 
     contract_rows = (((0,), (0,)), ((), ()))
     gathered_sum = lax.dot_general(

time: 93.2 us -> 110 us (1.18)
  waiting for transfers between devices: 45.9 us -> 65.6 us
  Pallas kernels: 8.15 us -> 5.42 us
  local copies, waits for them, and re-layouts: 1.07 us -> 3.78 us
  other arithmetic: 3.16 us -> 1.62 us
    ppermute x2 -> x4, waiting for transfers between devices: 18.2 us -> 44.8 us  [swapped(): return lax.ppermute(array, axis, [(i, i ^ 1) for i in range(count)])]
    ppermute x8, waiting for transfers between devices: 27.7 us -> 20.8 us  [passed_along(): lax.ppermute(array, axis, [(i, (i + by) % count) for i in range(count)])]
    ppermute x8, starting transfers between devices: 13.3 us -> 9.7 us  [passed_along(): lax.ppermute(array, axis, [(i, (i + by) % count) for i in range(count)])]
    ppermute x2 -> x4, starting transfers between devices: 6.95 us -> 9.82 us  [swapped(): return lax.ppermute(array, axis, [(i, i ^ 1) for i in range(count)])]
    squeeze x0 -> x2, local copies, waits for them, and re-layouts: none -> 2.78 us  [the longest x1 2.77 us: shards(): other_values = swapped(tile_values[1 - side], 'rep')]
    pallas_call x1, Pallas kernels: 8.15 us -> 5.42 us  [dense_block(): pl.pallas_call(kernel, grid_spec=pltpu.PrefetchScalarGridSpec(num_scalar_...]
    dot_general x4, matrix products: 4.99 us -> 7.25 us  [shards(): jnp.dot(blocks[k], slabs[k], preferred_element_type=jnp.float32)]
    convert_element_type x2 -> x0, other arithmetic: 1.86 us -> none  [the longest x1 1.38 us: activate(): scaled = (mask_rows.astype(jnp.float32)[:, None] * cot_rows.astype(jnp.fl...]
  transfers between devices with their start and end apart: 10 -> 12, of which waited for: 6 -> 5; matrix products, arithmetic and copies ran while one was open for 9% -> 8% of each run, Pallas kernels for 9% -> 5%
where the time goes in v3:
time: 110 us
  waiting for transfers between devices  65.6 us (60%)
  starting transfers between devices  19.5 us (18%)
  matrix products  12.7 us (12%)
  Pallas kernels  5.42 us (5%)
  local copies, waits for them, and re-layouts  3.78 us (3%)
  other arithmetic  1.62 us (1%)
    ppermute x4, waiting for transfers between devices, swapped(): return lax.ppermute(array, axis, [(i, i ^ 1) for i in range(count)])  44.8 us
    ppermute x8, waiting for transfers between devices, passed_along(): lax.ppermute(array, axis, [(i, (i + by) % count) for i in range(count)])  20.8 us
    ppermute x4, starting transfers between devices, swapped(): return lax.ppermute(array, axis, [(i, i ^ 1) for i in range(count)])  9.82 us
    ppermute x8, starting transfers between devices, passed_along(): lax.ppermute(array, axis, [(i, (i + by) % count) for i in range(count)])  9.7 us
    dot_general x4, matrix products, shards(): jnp.dot(blocks[k], slabs[k], preferred_element_type=jnp.float32)  7.25 us
    pallas_call x1, Pallas kernels, dense_block(): pl.pallas_call(kernel, grid_spec=pltpu.PrefetchScalarGridSpec(num_scalar_...  5.42 us
    squeeze x1, local copies, waits for them, and re-layouts, shards(): other_values = swapped(tile_values[1 - side], 'rep')  2.77 us
  transfers between devices with their start and end apart: 12, of which 5 were waited for; matrix products, arithmetic and copies ran while one was open for 8% of the time, Pallas kernels for 5%

profile of v3, /device:TPU:1, one launch (start us, length us, event | category | flops | bytes accessed | tf_op | source)
XLA Modules:
  0.0 109.5 jit_solution(9081560544325077397)
XLA Ops:
  0.6 0.0 copy-start
  0.6 0.0 copy-start.4
  0.7 0.0 copy-start.5
  0.7 2.8 %dynamic-slice_bitcast_fusion = (bf16[4,8,128,128]{3,2,1,0:T(8,128)(2,1)S(1)}, bf16[4,8,128,128]{3,2,1,0:T(8,128)(2,1)}) fusion(bf16[2,4,8,128,128]{4,3,2,1,0:T(8,128)(2,1)} %bitcast.23, s32[]{:T(128)S(6)} %select_n.46, s32[]{:T(128)S(6)} %select_n.45), kind=kLoop, calls=%fused_computation.17 | loop fusion | bytes 4194312 | tf_op jit(solution)/shard_map/squeeze | solution.py:77
  3.4 4.4 %collective-permute-start.1 = (bf16[4,8,128,128]{3,2,1,0:T(8,128)(2,1)S(1)}, bf16[4,8,128,128]{3,2,1,0:T(8,128)(2,1)S(1)}, u32[]{:S(2)}, u32[]{:S(2)}) collective-permute-start(bf16[4,8,128,128]{3,2,1,0:T(8,128)(2,1)S(1)} %get-tuple-element.2), channel_id=1, source_target_pairs={{0,1},{1,0},{2,3},{3,2},{4,5},{5,4},{6,7},{7,6},{8,9},{9,8},{10,11... | collective-permute-start | bytes 3145736 | tf_op jit(solution)/shard_map/ppermute | solution.py:18
  7.9 0.0 copy-done
  7.9 1.2 %convolution_convert_fusion.5 = bf16[1024,256]{1,0:T(8,128)(2,1)S(1)} fusion(bf16[1024,256]{1,0:T(8,128)(2,1)S(1)} %copy-done, bf16[256,256]{1,0:T(8,128)(2,1)} %param.8), kind=kOutput, calls=%fused_computation.9 | convolution fusion | flops 134479872 | bytes 1179648 | tf_op jit(solution)/shard_map/dot_general | solution.py:81
  9.1 1.0 collective-permute-start.4
  10.1 1.3 %collective-permute-start.3 = (bf16[1024,256]{1,0:T(8,128)(2,1)S(1)}, bf16[1024,256]{1,0:T(8,128)(2,1)}, u32[]{:S(2)}, u32[]{:S(2)}) collective-permute-start(bf16[1024,256]{1,0:T(8,128)(2,1)S(1)} %convolution_convert_fusion.5), channel_id=1, source_target_pairs={{0,2},{2,4},{4,6},{6,8},{8,10},{10,12},{12,14},{14,16},{16,18},{18... | collective-permute-start | bytes 1572872 | tf_op jit(solution)/shard_map/ppermute | solution.py:13
  11.4 1.3 %collective-permute-start.2 = (bf16[1024,256]{1,0:T(8,128)(2,1)S(1)}, bf16[1024,256]{1,0:T(8,128)(2,1)}, u32[]{:S(2)}, u32[]{:S(2)}) collective-permute-start(bf16[1024,256]{1,0:T(8,128)(2,1)S(1)} %convolution_convert_fusion.5), channel_id=1, source_target_pairs={{0,4},{2,6},{4,8},{6,10},{8,12},{10,14},{12,16},{14,18},{16,20},{1... | collective-permute-start | bytes 1572872 | tf_op jit(solution)/shard_map/ppermute | solution.py:13
  12.7 0.0 collective-permute-start
  12.7 0.1 dynamic-slice_convert_fusion
  12.8 34.9 %collective-permute-done = s32[4,8]{1,0:T(4,128)S(1)} collective-permute-done((s32[4,8]{1,0:T(4,128)S(1)}, s32[4,8]{1,0:T(4,128)S(1)}, u32[]{:S(2)}, u32[]{:S(2)}) %collective-permute-start) | collective-permute-done | bytes 160 | tf_op jit(solution)/shard_map/ppermute | solution.py:18
  47.7 0.0 collective-permute-start.5
  47.7 0.7 fusion.27.index_ref
  48.3 0.0 collective-permute-done.1.other_ref
  48.3 1.0 copy-done.2
  49.3 5.4 %shard_map.86 = bf16[512,5120]{1,0:T(8,128)(2,1)} custom-call(s32[4,16]{1,0:T(4,128)} %fusion.27.index_ref, bf16[4,8,128,128]{3,2,1,0:T(8,128)(2,1)} %get-tuple-element.3.own_ref, bf16[4,8,128,128]{3,2,1,0:T(8,128)(2,1)} %copy-done.2), custom_call_target="tpu_custom_call" | custom-call | tf_op jit(solution)/shard_map/pallas_call | solution.py:50
  54.7 0.0 collective-permute-done.4
  54.7 2.0 %fusion.12 = f32[512,256]{1,0:T(8,128)S(1)} fusion(bf16[1024,256]{1,0:T(8,128)(2,1)} %collective-permute-done.4, bf16[512,5120]{1,0:T(8,128)(2,1)} %shard_map.86), kind=kOutput, calls=%fused_computation.23 | convolution fusion | flops 268435456 | bytes 2097152 | tf_op jit(solution)/shard_map/dot_general | solution.py:97
  56.7 0.0 collective-permute-done.3
  56.7 2.0 %fusion.15 = f32[512,256]{1,0:T(8,128)S(1)} fusion(bf16[1024,256]{1,0:T(8,128)(2,1)} %collective-permute-done.3, bf16[512,5120]{1,0:T(8,128)(2,1)} %shard_map.86), kind=kOutput, calls=%fused_computation.26 | convolution fusion | flops 268435456 | bytes 2097152 | tf_op jit(solution)/shard_map/dot_general | solution.py:97
  58.7 0.0 collective-permute-done.2
  58.7 1.8 %fusion.18 = f32[512,256]{1,0:T(8,128)S(1)} fusion(bf16[1024,256]{1,0:T(8,128)(2,1)} %collective-permute-done.2, bf16[512,5120]{1,0:T(8,128)(2,1)} %shard_map.86), kind=kOutput, calls=%fused_computation.29 | convolution fusion | flops 268435456 | bytes 2097152 | tf_op jit(solution)/shard_map/dot_general | solution.py:97
  60.5 0.0 collective-permute-done.5
  60.6 0.0 copy-done.1
  60.6 1.5 %fusion.9 = f32[512,256]{1,0:T(8,128)S(1)} fusion(bf16[1024,256]{1,0:T(8,128)(2,1)} %collective-permute-done.5, bf16[512,5120]{1,0:T(8,128)(2,1)S(1)} %copy-done.1), kind=kOutput, calls=%fused_computation.20 | convolution fusion | flops 268435456 | bytes 2097152 | tf_op jit(solution)/shard_map/dot_general | solution.py:97
  62.1 0.7 multiply_convert_fusion
  62.8 0.5 convolution_convert_fusion.4
  63.2 0.5 convolution_convert_fusion.3
  63.7 0.0 copy-start.3
  63.7 0.5 convolution_convert_fusion.2
  64.2 0.5 convolution_convert_fusion.1
  64.6 4.0 %collective-permute-start.7 = (bf16[256,1024]{1,0:T(8,128)(2,1)S(1)}, bf16[256,1024]{1,0:T(8,128)(2,1)S(1)}, u32[]{:S(2)}, u32[]{:S(2)}) collective-permute-start(bf16[256,1024]{1,0:T(8,128)(2,1)S(1)} %convolution_convert_fusion.4), channel_id=1, source_target_pairs={{0,124},{2,126},{4,0},{6,2},{8,4},{10,6},{12,8},{14,10},{16,12},{1... | collective-permute-start | bytes 1572872 | tf_op jit(solution)/shard_map/ppermute | solution.py:13
  68.6 2.1 %collective-permute-start.8 = (bf16[256,1024]{1,0:T(8,128)(2,1)S(1)}, bf16[256,1024]{1,0:T(8,128)(2,1)S(1)}, u32[]{:S(2)}, u32[]{:S(2)}) collective-permute-start(bf16[256,1024]{1,0:T(8,128)(2,1)S(1)} %convolution_convert_fusion.3), channel_id=1, source_target_pairs={{0,126},{2,0},{4,2},{6,4},{8,6},{10,8},{12,10},{14,12},{16,14},{18... | collective-permute-start | bytes 1572872 | tf_op jit(solution)/shard_map/ppermute | solution.py:13
  70.7 0.0 collective-permute-start.9
  70.7 0.0 collective-permute-start.10
  70.7 2.7 %collective-permute-start.6 = (bf16[512,256]{1,0:T(8,128)(2,1)S(1)}, bf16[512,256]{1,0:T(8,128)(2,1)S(1)}, u32[]{:S(2)}, u32[]{:S(2)}) collective-permute-start(bf16[512,256]{1,0:T(8,128)(2,1)S(1)} %get-tuple-element.5), channel_id=1, source_target_pairs={{0,1},{1,0},{2,3},{3,2},{4,5},{5,4},{6,7},{7,6},{8,9},{9,8},{10,11... | collective-permute-start | bytes 786440 | tf_op jit(solution)/shard_map/ppermute | solution.py:18
  73.4 4.6 %collective-permute-done.7 = bf16[256,1024]{1,0:T(8,128)(2,1)S(1)} collective-permute-done((bf16[256,1024]{1,0:T(8,128)(2,1)S(1)}, bf16[256,1024]{1,0:T(8,128)(2,1)S(1)}, u32[]{:S(2)}, u32[]{:S(2)}) %collective-permute-start.7) | collective-permute-done | bytes 524320 | tf_op jit(solution)/shard_map/ppermute | solution.py:13
  78.0 6.3 %collective-permute-done.8 = bf16[256,1024]{1,0:T(8,128)(2,1)S(1)} collective-permute-done((bf16[256,1024]{1,0:T(8,128)(2,1)S(1)}, bf16[256,1024]{1,0:T(8,128)(2,1)S(1)}, u32[]{:S(2)}, u32[]{:S(2)}) %collective-permute-start.8) | collective-permute-done | bytes 524320 | tf_op jit(solution)/shard_map/ppermute | solution.py:13
  84.2 0.0 collective-permute-done.9
  84.3 9.9 %collective-permute-done.10 = bf16[256,1024]{1,0:T(8,128)(2,1)S(1)} collective-permute-done((bf16[256,1024]{1,0:T(8,128)(2,1)S(1)}, bf16[256,1024]{1,0:T(8,128)(2,1)S(1)}, u32[]{:S(2)}, u32[]{:S(2)}) %collective-permute-start.10) | collective-permute-done | bytes 524320 | tf_op jit(solution)/shard_map/ppermute | solution.py:13
  94.2 0.6 fusion.3
  94.8 2.7 %collective-permute-start.11 = (bf16[256,1024]{1,0:T(8,128)(2,1)S(1)}, bf16[256,1024]{1,0:T(8,128)(2,1)S(1)}, u32[]{:S(2)}, u32[]{:S(2)}) collective-permute-start(bf16[256,1024]{1,0:T(8,128)(2,1)S(1)} %fusion.3), channel_id=1, source_target_pairs={{0,1},{1,0},{2,3},{3,2},{4,5},{5,4},{6,7},{7,6},{8,9},{9,8},{10,11... | collective-permute-start | bytes 1572872 | tf_op jit(solution)/shard_map/ppermute | solution.py:18
  97.6 0.0 collective-permute-done.6
  97.6 0.8 pad_maximum_fusion
  98.4 9.9 %collective-permute-done.11 = bf16[256,1024]{1,0:T(8,128)(2,1)S(1)} collective-permute-done((bf16[256,1024]{1,0:T(8,128)(2,1)S(1)}, bf16[256,1024]{1,0:T(8,128)(2,1)S(1)}, u32[]{:S(2)}, u32[]{:S(2)}) %collective-permute-start.11) | collective-permute-done | bytes 524320 | tf_op jit(solution)/shard_map/ppermute | solution.py:18
  108.4 1.2 %convolution_convert_fusion = bf16[1024,256]{1,0:T(8,128)(2,1)} fusion(bf16[256,256]{1,0:T(8,128)(2,1)S(1)} %copy-done.3, bf16[256,1024]{1,0:T(8,128)(2,1)S(1)} %collective-permute-done.11, bf16[256,1024]{1,0:T(8,128)(2,1)S(1)} %fusion.3), kind=kOutput, calls=%fused_computation.4 | convolution fusion | flops 135528448 | bytes 1703936 | tf_op jit(solution)/shard_map/dot_general | solution.py:122
  (11 shorter events, 0.1 us)
Async XLA Ops:
  0.6 7.2 %copy-start = (bf16[1024,256]{1,0:T(8,128)(2,1)S(1)}, bf16[1024,256]{1,0:T(8,128)(2,1)}, u32[]{:S(2)}) copy-start(bf16[1024,256]{1,0:T(8,128)(2,1)} %param.7) | copy-start | bytes 1572868
  0.6 12.0 %copy-start.4 = (s32[8,8]{1,0:T(8,128)S(1)}, s32[8,8]{1,0:T(8,128)}, u32[]{:S(2)}) copy-start(s32[8,8]{1,0:T(8,128)} %param.12) | copy-start | bytes 772
  0.7 12.0 %copy-start.5 = (s32[1024]{0:T(1024)S(1)}, s32[1024]{0:T(1024)}, u32[]{:S(2)}) copy-start(s32[1024]{0:T(1024)} %param.11) | copy-start | bytes 12292
  3.4 44.9 %collective-permute-start.1 = (bf16[4,8,128,128]{3,2,1,0:T(8,128)(2,1)S(1)}, bf16[4,8,128,128]{3,2,1,0:T(8,128)(2,1)S(1)}, u32[]{:S(2)}, u32[]{:S(2)}) collective-permute-start(bf16[4,8,128,128]{3,2,1,0:T(8,128)(2,1)S(1)} %get-tuple-element.2), channel_id=1, source_target_pairs={{0,1},{1,0},{2,3},{3,2},{4,5},{5,4},{6,7},{7,6},{8,9},{9,8},{10,11... | collective-permute-start | bytes 3145736 | tf_op jit(solution)/shard_map/ppermute | solution.py:18
  9.1 45.6 %collective-permute-start.4 = (bf16[1024,256]{1,0:T(8,128)(2,1)S(1)}, bf16[1024,256]{1,0:T(8,128)(2,1)}, u32[]{:S(2)}, u32[]{:S(2)}) collective-permute-start(bf16[1024,256]{1,0:T(8,128)(2,1)S(1)} %convolution_convert_fusion.5), channel_id=1, source_target_pairs={{0,126},{2,0},{4,2},{6,4},{8,6},{10,8},{12,10},{14,12},{16,14},{18... | collective-permute-start | bytes 1572872 | tf_op jit(solution)/shard_map/ppermute | solution.py:13
  10.1 46.6 %collective-permute-start.3 = (bf16[1024,256]{1,0:T(8,128)(2,1)S(1)}, bf16[1024,256]{1,0:T(8,128)(2,1)}, u32[]{:S(2)}, u32[]{:S(2)}) collective-permute-start(bf16[1024,256]{1,0:T(8,128)(2,1)S(1)} %convolution_convert_fusion.5), channel_id=1, source_target_pairs={{0,2},{2,4},{4,6},{6,8},{8,10},{10,12},{12,14},{14,16},{16,18},{18... | collective-permute-start | bytes 1572872 | tf_op jit(solution)/shard_map/ppermute | solution.py:13
  11.4 47.4 %collective-permute-start.2 = (bf16[1024,256]{1,0:T(8,128)(2,1)S(1)}, bf16[1024,256]{1,0:T(8,128)(2,1)}, u32[]{:S(2)}, u32[]{:S(2)}) collective-permute-start(bf16[1024,256]{1,0:T(8,128)(2,1)S(1)} %convolution_convert_fusion.5), channel_id=1, source_target_pairs={{0,4},{2,6},{4,8},{6,10},{8,12},{10,14},{12,16},{14,18},{16,20},{1... | collective-permute-start | bytes 1572872 | tf_op jit(solution)/shard_map/ppermute | solution.py:13
  12.7 35.0 %collective-permute-start = (s32[4,8]{1,0:T(4,128)S(1)}, s32[4,8]{1,0:T(4,128)S(1)}, u32[]{:S(2)}, u32[]{:S(2)}) collective-permute-start(s32[4,8]{1,0:T(4,128)S(1)} %get-tuple-element.9), channel_id=1, source_target_pairs={{0,1},{1,0},{2,3},{3,2},{4,5},{5,4},{6,7},{7,6},{8,9},{9,8},{10,11... | collective-permute-start | bytes 392 | tf_op jit(solution)/shard_map/ppermute | solution.py:18
  47.7 12.9 %collective-permute-start.5 = (bf16[1024,256]{1,0:T(8,128)(2,1)S(1)}, bf16[1024,256]{1,0:T(8,128)(2,1)}, u32[]{:S(2)}, u32[]{:S(2)}) collective-permute-start(bf16[1024,256]{1,0:T(8,128)(2,1)S(1)} %convolution_convert_fusion.5), channel_id=1, source_target_pairs={{0,124},{2,126},{4,0},{6,2},{8,4},{10,6},{12,8},{14,10},{16,12},{1... | collective-permute-start | bytes 1572872 | tf_op jit(solution)/shard_map/ppermute | solution.py:13
  48.3 1.0 copy-start.2
  54.7 5.8 %copy-start.1 = (bf16[512,5120]{1,0:T(8,128)(2,1)S(1)}, bf16[512,5120]{1,0:T(8,128)(2,1)}, u32[]{:S(2)}) copy-start(bf16[512,5120]{1,0:T(8,128)(2,1)} %shard_map.86) | copy-start | bytes 15728644
  54.7 7.3 %copy-start.6 = (bf16[1024,256]{1,0:T(8,128)(2,1)S(1)}, bf16[1024,256]{1,0:T(8,128)(2,1)}, u32[]{:S(2)}) copy-start(bf16[1024,256]{1,0:T(8,128)(2,1)} %param.10) | copy-start | bytes 1572868
  54.7 7.4 %copy-start.7 = (f32[256]{0:T(256)S(1)}, f32[256]{0:T(256)}, u32[]{:S(2)}) copy-start(f32[256]{0:T(256)} %param.9) | copy-start | bytes 3076
  63.7 44.7 %copy-start.3 = (bf16[256,256]{1,0:T(8,128)(2,1)S(1)}, bf16[256,256]{1,0:T(8,128)(2,1)}, u32[]{:S(2)}) copy-start(bf16[256,256]{1,0:T(8,128)(2,1)} %param.8) | copy-start | bytes 393220
  64.6 13.3 %collective-permute-start.7 = (bf16[256,1024]{1,0:T(8,128)(2,1)S(1)}, bf16[256,1024]{1,0:T(8,128)(2,1)S(1)}, u32[]{:S(2)}, u32[]{:S(2)}) collective-permute-start(bf16[256,1024]{1,0:T(8,128)(2,1)S(1)} %convolution_convert_fusion.4), channel_id=1, source_target_pairs={{0,124},{2,126},{4,0},{6,2},{8,4},{10,6},{12,8},{14,10},{16,12},{1... | collective-permute-start | bytes 1572872 | tf_op jit(solution)/shard_map/ppermute | solution.py:13
  68.6 15.7 %collective-permute-start.8 = (bf16[256,1024]{1,0:T(8,128)(2,1)S(1)}, bf16[256,1024]{1,0:T(8,128)(2,1)S(1)}, u32[]{:S(2)}, u32[]{:S(2)}) collective-permute-start(bf16[256,1024]{1,0:T(8,128)(2,1)S(1)} %convolution_convert_fusion.3), channel_id=1, source_target_pairs={{0,126},{2,0},{4,2},{6,4},{8,6},{10,8},{12,10},{14,12},{16,14},{18... | collective-permute-start | bytes 1572872 | tf_op jit(solution)/shard_map/ppermute | solution.py:13
  70.7 13.5 %collective-permute-start.9 = (bf16[256,1024]{1,0:T(8,128)(2,1)S(1)}, bf16[256,1024]{1,0:T(8,128)(2,1)S(1)}, u32[]{:S(2)}, u32[]{:S(2)}) collective-permute-start(bf16[256,1024]{1,0:T(8,128)(2,1)S(1)} %convolution_convert_fusion.2), channel_id=1, source_target_pairs={{0,2},{2,4},{4,6},{6,8},{8,10},{10,12},{12,14},{14,16},{16,18},{18... | collective-permute-start | bytes 1572872 | tf_op jit(solution)/shard_map/ppermute | solution.py:13
  70.7 23.5 %collective-permute-start.10 = (bf16[256,1024]{1,0:T(8,128)(2,1)S(1)}, bf16[256,1024]{1,0:T(8,128)(2,1)S(1)}, u32[]{:S(2)}, u32[]{:S(2)}) collective-permute-start(bf16[256,1024]{1,0:T(8,128)(2,1)S(1)} %convolution_convert_fusion.1), channel_id=1, source_target_pairs={{0,4},{2,6},{4,8},{6,10},{8,12},{10,14},{12,16},{14,18},{16,20},{1... | collective-permute-start | bytes 1572872 | tf_op jit(solution)/shard_map/ppermute | solution.py:13
  70.7 26.8 %collective-permute-start.6 = (bf16[512,256]{1,0:T(8,128)(2,1)S(1)}, bf16[512,256]{1,0:T(8,128)(2,1)S(1)}, u32[]{:S(2)}, u32[]{:S(2)}) collective-permute-start(bf16[512,256]{1,0:T(8,128)(2,1)S(1)} %get-tuple-element.5), channel_id=1, source_target_pairs={{0,1},{1,0},{2,3},{3,2},{4,5},{5,4},{6,7},{7,6},{8,9},{9,8},{10,11... | collective-permute-start | bytes 786440 | tf_op jit(solution)/shard_map/ppermute | solution.py:18
  94.8 13.5 %collective-permute-start.11 = (bf16[256,1024]{1,0:T(8,128)(2,1)S(1)}, bf16[256,1024]{1,0:T(8,128)(2,1)S(1)}, u32[]{:S(2)}, u32[]{:S(2)}) collective-permute-start(bf16[256,1024]{1,0:T(8,128)(2,1)S(1)} %fusion.3), channel_id=1, source_target_pairs={{0,1},{1,0},{2,3},{3,2},{4,5},{5,4},{6,7},{7,6},{8,9},{9,8},{10,11... | collective-permute-start | bytes 1572872 | tf_op jit(solution)/shard_map/ppermute | solution.py:18

commit v4 on v2

--- a/solution.py
+++ b/solution.py
@@ -6,6 +6,9 @@
 from jax.sharding import PartitionSpec as P
 
 REACH = 2
+FWD_T = jnp.float32
+PIECE_T = jnp.float32
+BACK_T = jnp.float32
 
 
 def passed_along(array, axis, by):
@@ -82,7 +85,7 @@
     for k in range(span):
         if k != REACH:
             partial_value = partial_value + jnp.dot(blocks[k], slabs[k], preferred_element_type=jnp.float32)
-    partial_value = partial_value.astype(jnp.bfloat16)
+    partial_value = partial_value.astype(FWD_T)
     preact = (
         partial_value.astype(jnp.float32) + swapped(partial_value, "rep").astype(jnp.float32)
     ) + bias
@@ -96,10 +99,10 @@
         shift = k - REACH
         if shift != 0:
             piece = lax.dot_general(scaled, blocks[k], contract_rows, preferred_element_type=jnp.float32)
-            gathered_sum = gathered_sum + passed_along(piece.astype(jnp.bfloat16), "blk", shift).astype(
+            gathered_sum = gathered_sum + passed_along(piece.astype(PIECE_T), "blk", shift).astype(
                 jnp.float32
             )
-    gathered_sum = gathered_sum.astype(jnp.bfloat16)
+    gathered_sum = gathered_sum.astype(BACK_T)
     back_sum_t = (
         gathered_sum.astype(jnp.float32) + swapped(gathered_sum, "rep").astype(jnp.float32)
     ).astype(jnp.bfloat16)

time: 93.2 us -> 133 us (1.43)
  waiting for transfers between devices: 45.9 us -> 85.8 us
    ppermute x2, waiting for transfers between devices: 18.2 us -> 40.4 us  [swapped(): return lax.ppermute(array, axis, [(i, i ^ 1) for i in range(count)])]
    ppermute x8, waiting for transfers between devices: 27.7 us -> 45.4 us  [passed_along(): lax.ppermute(array, axis, [(i, (i + by) % count) for i in range(count)])]
  transfers between devices with their start and end apart: 10 -> 10, of which waited for: 6 -> 6; matrix products, arithmetic and copies ran while one was open for 9% -> 6% of each run, Pallas kernels for 9% -> 6%
where the time goes in v4:
time: 133 us; the launch traced here: 132 us
  waiting for transfers between devices  85.8 us (65%)
  starting transfers between devices  20.2 us (15%)
  matrix products  13.6 us (10%)
  Pallas kernels  8.13 us (6%)
  other arithmetic  2.65 us (2%)
    ppermute x8, waiting for transfers between devices, passed_along(): lax.ppermute(array, axis, [(i, (i + by) % count) for i in range(count)])  45.4 us
    ppermute x2, waiting for transfers between devices, swapped(): return lax.ppermute(array, axis, [(i, i ^ 1) for i in range(count)])  40.4 us
    ppermute x8, starting transfers between devices, passed_along(): lax.ppermute(array, axis, [(i, (i + by) % count) for i in range(count)])  13.3 us
    pallas_call x1, Pallas kernels, dense_block(): pl.pallas_call(kernel, grid_spec=pltpu.PrefetchScalarGridSpec(num_scalar_...  8.13 us
    ppermute x2, starting transfers between devices, swapped(): return lax.ppermute(array, axis, [(i, i ^ 1) for i in range(count)])  6.87 us
    dot_general x4, matrix products, shards(): jnp.dot(blocks[k], slabs[k], preferred_element_type=jnp.float32)  4.99 us
    dot_general x4, matrix products, shards(): lax.dot_general(scaled, blocks[k], contract_rows, preferred_element_type=...  2.9 us
  transfers between devices with their start and end apart: 10, of which 6 were waited for; matrix products, arithmetic and copies ran while one was open for 6% of the time, Pallas kernels for 6%

profile of v4, /device:TPU:1, one launch (start us, length us, event | category | flops | bytes accessed | tf_op | source)
XLA Modules:
  0.0 132.2 jit_solution(4771113066631150376)
XLA Ops:
  0.6 0.0 copy-start
  0.6 1.0 copy-done
  1.7 1.2 convolution_convert_fusion.1
  2.9 7.2 %collective-permute-start.3 = (bf16[1024,256]{1,0:T(8,128)(2,1)S(1)}, bf16[1024,256]{1,0:T(8,128)(2,1)S(1)}, u32[]{:S(2)}, u32[]{:S(2)}) collective-permute-start(bf16[1024,256]{1,0:T(8,128)(2,1)S(1)} %convolution_convert_fusion.1), channel_id=1, source_target_pairs={{0,124},{2,126},{4,0},{6,2},{8,4},{10,6},{12,8},{14,10},{16,12},{1... | collective-permute-start | bytes 1572872 | tf_op jit(solution)/shard_map/ppermute | solution.py:16
  10.1 1.0 collective-permute-start.2
  11.0 0.8 collective-permute-start.1
  11.8 0.0 collective-permute-start
  11.8 1.3 fusion.49.index_ref
  13.1 8.1 %shard_map.86 = bf16[1024,5120]{1,0:T(8,128)(2,1)} custom-call(s32[8,8]{1,0:T(8,128)} %fusion.49.index_ref, bf16[8,8,128,128]{3,2,1,0:T(8,128)(2,1)} %values_ref.1), custom_call_target="tpu_custom_call" | custom-call | tf_op jit(solution)/shard_map/pallas_call | solution.py:51
  21.2 0.0 copy-start.1
  21.2 2.5 %fusion.18 = f32[1024,256]{1,0:T(8,128)S(1)} fusion(bf16[1024,256]{1,0:T(8,128)(2,1)S(1)} %convolution_convert_fusion.1, bf16[1024,5120]{1,0:T(8,128)(2,1)} %shard_map.86), kind=kOutput, calls=%fused_computation.18 | convolution fusion | flops 536870912 | bytes 3670016 | tf_op jit(solution)/shard_map/dot_general | solution.py:84
  23.7 0.0 collective-permute-done.3
  23.7 2.8 %fusion.2 = f32[1024,256]{1,0:T(8,128)S(1)} fusion(bf16[1024,256]{1,0:T(8,128)(2,1)S(1)} %collective-permute-done.3, bf16[1024,5120]{1,0:T(8,128)(2,1)} %shard_map.86), kind=kOutput, calls=%fused_computation.2 | convolution fusion | flops 536870912 | bytes 3670016 | tf_op jit(solution)/shard_map/dot_general | solution.py:87
  26.6 0.0 copy-start.4
  26.6 0.0 copy-start.2
  26.6 0.0 copy-start.5
  26.6 0.0 collective-permute-done.2
  26.6 0.0 copy-done.1
  26.6 0.7 fusion.6
  27.3 0.0 collective-permute-done.1
  27.3 0.7 fusion.10
  28.1 6.3 %collective-permute-done = bf16[1024,256]{1,0:T(8,128)(2,1)S(1)} collective-permute-done((bf16[1024,256]{1,0:T(8,128)(2,1)S(1)}, bf16[1024,256]{1,0:T(8,128)(2,1)S(1)}, u32[]{:S(2)}, u32[]{:S(2)}) %collective-permute-start) | collective-permute-done | bytes 524320 | tf_op jit(solution)/shard_map/ppermute | solution.py:16
  34.4 0.7 fusion.41
  35.1 3.5 %collective-permute-start.4 = (f32[1024,256]{1,0:T(8,128)S(1)}, f32[1024,256]{1,0:T(8,128)S(1)}, u32[]{:S(2)}, u32[]{:S(2)}) collective-permute-start(f32[1024,256]{1,0:T(8,128)S(1)} %fusion.41), channel_id=1, source_target_pairs={{0,1},{1,0},{2,3},{3,2},{4,5},{5,4},{6,7},{7,6},{8,9},{9,8},{10,11... | collective-permute-start | bytes 3145736 | tf_op jit(solution)/shard_map/ppermute | solution.py:21
  38.6 0.0 copy-done.4
  38.6 20.2 %collective-permute-done.4 = f32[1024,256]{1,0:T(8,128)S(1)} collective-permute-done((f32[1024,256]{1,0:T(8,128)S(1)}, f32[1024,256]{1,0:T(8,128)S(1)}, u32[]{:S(2)}, u32[]{:S(2)}) %collective-permute-start.4) | collective-permute-done | bytes 1048608 | tf_op jit(solution)/shard_map/ppermute | solution.py:21
  58.8 0.0 copy-done.2
  58.8 0.0 copy-done.5
  58.8 1.3 %multiply_convert_fusion = (bf16[1024,256]{1,0:T(8,128)(2,1)S(1)}, bf16[1024,256]{1,0:T(8,128)(2,1)}) fusion(bf16[1024,256]{1,0:T(8,128)(2,1)S(1)} %copy-done.2, f32[1024]{0:T(1024)S(1)} %convert_element_type.23, f32[256]{0:T(256)S(1)} %copy-done.5, f32[1024,256]{1,0:T(8,128)S(1)} %fusion.41, f32[1024,256]{1,0:T(8,128)S(1)} %collective-permute-done.4), kind=kLoop, calls=%fused_computation.31 | loop fusion | flops 3932160 | bytes 3675136 | tf_op jit(solution)/shard_map/convert_element_type | solution.py:33
  60.2 0.0 copy-start.3
  60.2 0.7 fusion
  60.9 0.7 fusion.4
  61.6 0.7 fusion.8
  62.4 0.7 fusion.12
  63.1 2.7 %collective-permute-start.5 = (f32[256,1024]{1,0:T(8,128)S(1)}, f32[256,1024]{1,0:T(8,128)S(1)}, u32[]{:S(2)}, u32[]{:S(2)}) collective-permute-start(f32[256,1024]{1,0:T(8,128)S(1)} %fusion.12), channel_id=1, source_target_pairs={{0,124},{2,126},{4,0},{6,2},{8,4},{10,6},{12,8},{14,10},{16,12},{1... | collective-permute-start | bytes 3145736 | tf_op jit(solution)/shard_map/ppermute | solution.py:16
  65.8 0.2 collective-permute-start.6
  66.0 1.5 %collective-permute-start.7 = (f32[256,1024]{1,0:T(8,128)S(1)}, f32[256,1024]{1,0:T(8,128)S(1)}, u32[]{:S(2)}, u32[]{:S(2)}) collective-permute-start(f32[256,1024]{1,0:T(8,128)S(1)} %fusion.4), channel_id=1, source_target_pairs={{0,2},{2,4},{4,6},{6,8},{8,10},{10,12},{12,14},{14,16},{16,18},{18... | collective-permute-start | bytes 3145736 | tf_op jit(solution)/shard_map/ppermute | solution.py:16
  67.5 0.0 collective-permute-start.8
  67.5 20.9 %collective-permute-done.5 = f32[256,1024]{1,0:T(8,128)S(1)} collective-permute-done((f32[256,1024]{1,0:T(8,128)S(1)}, f32[256,1024]{1,0:T(8,128)S(1)}, u32[]{:S(2)}, u32[]{:S(2)}) %collective-permute-start.5) | collective-permute-done | bytes 1048608 | tf_op jit(solution)/shard_map/ppermute | solution.py:16
  88.4 8.7 %collective-permute-done.6 = f32[256,1024]{1,0:T(8,128)S(1)} collective-permute-done((f32[256,1024]{1,0:T(8,128)S(1)}, f32[256,1024]{1,0:T(8,128)S(1)}, u32[]{:S(2)}, u32[]{:S(2)}) %collective-permute-start.6) | collective-permute-done | bytes 1048608 | tf_op jit(solution)/shard_map/ppermute | solution.py:16
  97.2 0.0 collective-permute-done.7
  97.2 9.4 %collective-permute-done.8 = f32[256,1024]{1,0:T(8,128)S(1)} collective-permute-done((f32[256,1024]{1,0:T(8,128)S(1)}, f32[256,1024]{1,0:T(8,128)S(1)}, u32[]{:S(2)}, u32[]{:S(2)}) %collective-permute-start.8) | collective-permute-done | bytes 1048608 | tf_op jit(solution)/shard_map/ppermute | solution.py:16
  106.6 0.8 fusion.29
  107.3 3.4 %collective-permute-start.9 = (f32[256,1024]{1,0:T(8,128)S(1)}, f32[256,1024]{1,0:T(8,128)S(1)}, u32[]{:S(2)}, u32[]{:S(2)}) collective-permute-start(f32[256,1024]{1,0:T(8,128)S(1)} %fusion.29), channel_id=1, source_target_pairs={{0,1},{1,0},{2,3},{3,2},{4,5},{5,4},{6,7},{7,6},{8,9},{9,8},{10,11... | collective-permute-start | bytes 3145736 | tf_op jit(solution)/shard_map/ppermute | solution.py:21
  110.7 20.2 %collective-permute-done.9 = f32[256,1024]{1,0:T(8,128)S(1)} collective-permute-done((f32[256,1024]{1,0:T(8,128)S(1)}, f32[256,1024]{1,0:T(8,128)S(1)}, u32[]{:S(2)}, u32[]{:S(2)}) %collective-permute-start.9) | collective-permute-done | bytes 1048608 | tf_op jit(solution)/shard_map/ppermute | solution.py:21
  130.9 0.0 copy-done.3
  130.9 1.3 convolution_convert_fusion
  (1 shorter events, 0.0 us)
Async XLA Ops:
  0.6 1.0 copy-start
  2.9 20.8 %collective-permute-start.3 = (bf16[1024,256]{1,0:T(8,128)(2,1)S(1)}, bf16[1024,256]{1,0:T(8,128)(2,1)S(1)}, u32[]{:S(2)}, u32[]{:S(2)}) collective-permute-start(bf16[1024,256]{1,0:T(8,128)(2,1)S(1)} %convolution_convert_fusion.1), channel_id=1, source_target_pairs={{0,124},{2,126},{4,0},{6,2},{8,4},{10,6},{12,8},{14,10},{16,12},{1... | collective-permute-start | bytes 1572872 | tf_op jit(solution)/shard_map/ppermute | solution.py:16
  10.1 16.5 %collective-permute-start.2 = (bf16[1024,256]{1,0:T(8,128)(2,1)S(1)}, bf16[1024,256]{1,0:T(8,128)(2,1)S(1)}, u32[]{:S(2)}, u32[]{:S(2)}) collective-permute-start(bf16[1024,256]{1,0:T(8,128)(2,1)S(1)} %convolution_convert_fusion.1), channel_id=1, source_target_pairs={{0,126},{2,0},{4,2},{6,4},{8,6},{10,8},{12,10},{14,12},{16,14},{18... | collective-permute-start | bytes 1572872 | tf_op jit(solution)/shard_map/ppermute | solution.py:16
  11.0 16.3 %collective-permute-start.1 = (bf16[1024,256]{1,0:T(8,128)(2,1)S(1)}, bf16[1024,256]{1,0:T(8,128)(2,1)S(1)}, u32[]{:S(2)}, u32[]{:S(2)}) collective-permute-start(bf16[1024,256]{1,0:T(8,128)(2,1)S(1)} %convolution_convert_fusion.1), channel_id=1, source_target_pairs={{0,2},{2,4},{4,6},{6,8},{8,10},{10,12},{12,14},{14,16},{16,18},{18... | collective-permute-start | bytes 1572872 | tf_op jit(solution)/shard_map/ppermute | solution.py:16
  11.8 22.6 %collective-permute-start = (bf16[1024,256]{1,0:T(8,128)(2,1)S(1)}, bf16[1024,256]{1,0:T(8,128)(2,1)S(1)}, u32[]{:S(2)}, u32[]{:S(2)}) collective-permute-start(bf16[1024,256]{1,0:T(8,128)(2,1)S(1)} %convolution_convert_fusion.1), channel_id=1, source_target_pairs={{0,4},{2,6},{4,8},{6,10},{8,12},{10,14},{12,16},{14,18},{16,20},{1... | collective-permute-start | bytes 1572872 | tf_op jit(solution)/shard_map/ppermute | solution.py:16
  21.2 5.4 %copy-start.1 = (bf16[1024,5120]{1,0:T(8,128)(2,1)S(1)}, bf16[1024,5120]{1,0:T(8,128)(2,1)}, u32[]{:S(2)}) copy-start(bf16[1024,5120]{1,0:T(8,128)(2,1)} %shard_map.86) | copy-start | bytes 31457284
  26.6 12.0 %copy-start.4 = (s32[1024]{0:T(1024)S(1)}, s32[1024]{0:T(1024)}, u32[]{:S(2)}) copy-start(s32[1024]{0:T(1024)} %param.11) | copy-start | bytes 12292
  26.6 32.3 %copy-start.2 = (bf16[1024,256]{1,0:T(8,128)(2,1)S(1)}, bf16[1024,256]{1,0:T(8,128)(2,1)}, u32[]{:S(2)}) copy-start(bf16[1024,256]{1,0:T(8,128)(2,1)} %param.10) | copy-start | bytes 1572868
  26.6 32.3 %copy-start.5 = (f32[256]{0:T(256)S(1)}, f32[256]{0:T(256)}, u32[]{:S(2)}) copy-start(f32[256]{0:T(256)} %param.9) | copy-start | bytes 3076
  35.1 23.7 %collective-permute-start.4 = (f32[1024,256]{1,0:T(8,128)S(1)}, f32[1024,256]{1,0:T(8,128)S(1)}, u32[]{:S(2)}, u32[]{:S(2)}) collective-permute-start(f32[1024,256]{1,0:T(8,128)S(1)} %fusion.41), channel_id=1, source_target_pairs={{0,1},{1,0},{2,3},{3,2},{4,5},{5,4},{6,7},{7,6},{8,9},{9,8},{10,11... | collective-permute-start | bytes 3145736 | tf_op jit(solution)/shard_map/ppermute | solution.py:21
  60.2 70.7 %copy-start.3 = (bf16[256,256]{1,0:T(8,128)(2,1)S(1)}, bf16[256,256]{1,0:T(8,128)(2,1)}, u32[]{:S(2)}) copy-start(bf16[256,256]{1,0:T(8,128)(2,1)} %param.8) | copy-start | bytes 393220
  63.1 25.3 %collective-permute-start.5 = (f32[256,1024]{1,0:T(8,128)S(1)}, f32[256,1024]{1,0:T(8,128)S(1)}, u32[]{:S(2)}, u32[]{:S(2)}) collective-permute-start(f32[256,1024]{1,0:T(8,128)S(1)} %fusion.12), channel_id=1, source_target_pairs={{0,124},{2,126},{4,0},{6,2},{8,4},{10,6},{12,8},{14,10},{16,12},{1... | collective-permute-start | bytes 3145736 | tf_op jit(solution)/shard_map/ppermute | solution.py:16
  65.8 31.4 %collective-permute-start.6 = (f32[256,1024]{1,0:T(8,128)S(1)}, f32[256,1024]{1,0:T(8,128)S(1)}, u32[]{:S(2)}, u32[]{:S(2)}) collective-permute-start(f32[256,1024]{1,0:T(8,128)S(1)} %fusion.8), channel_id=1, source_target_pairs={{0,126},{2,0},{4,2},{6,4},{8,6},{10,8},{12,10},{14,12},{16,14},{18... | collective-permute-start | bytes 3145736 | tf_op jit(solution)/shard_map/ppermute | solution.py:16
  66.0 31.2 %collective-permute-start.7 = (f32[256,1024]{1,0:T(8,128)S(1)}, f32[256,1024]{1,0:T(8,128)S(1)}, u32[]{:S(2)}, u32[]{:S(2)}) collective-permute-start(f32[256,1024]{1,0:T(8,128)S(1)} %fusion.4), channel_id=1, source_target_pairs={{0,2},{2,4},{4,6},{6,8},{8,10},{10,12},{12,14},{14,16},{16,18},{18... | collective-permute-start | bytes 3145736 | tf_op jit(solution)/shard_map/ppermute | solution.py:16
  67.5 39.1 %collective-permute-start.8 = (f32[256,1024]{1,0:T(8,128)S(1)}, f32[256,1024]{1,0:T(8,128)S(1)}, u32[]{:S(2)}, u32[]{:S(2)}) collective-permute-start(f32[256,1024]{1,0:T(8,128)S(1)} %fusion), channel_id=1, source_target_pairs={{0,4},{2,6},{4,8},{6,10},{8,12},{10,14},{12,16},{14,18},{16,20},{1... | collective-permute-start | bytes 3145736 | tf_op jit(solution)/shard_map/ppermute | solution.py:16
  107.3 23.6 %collective-permute-start.9 = (f32[256,1024]{1,0:T(8,128)S(1)}, f32[256,1024]{1,0:T(8,128)S(1)}, u32[]{:S(2)}, u32[]{:S(2)}) collective-permute-start(f32[256,1024]{1,0:T(8,128)S(1)} %fusion.29), channel_id=1, source_target_pairs={{0,1},{1,0},{2,3},{3,2},{4,5},{5,4},{6,7},{7,6},{8,9},{9,8},{10,11... | collective-permute-start | bytes 3145736 | tf_op jit(solution)/shard_map/ppermute | solution.py:21

commit v5 on v2

--- a/solution.py
+++ b/solution.py
@@ -11,6 +11,13 @@
 def passed_along(array, axis, by):
     count = lax.axis_size(axis)
     return lax.ppermute(array, axis, [(i, (i + by) % count) for i in range(count)])
+
+
+def paired(array, axis, even_by, odd_by):
+    count = lax.axis_size(axis)
+    return lax.ppermute(
+        array, axis, [(i, (i + (even_by if i % 2 == 0 else odd_by)) % count) for i in range(count)]
+    )
 
 
 def swapped(array, axis):
@@ -66,43 +73,40 @@
     span = 2 * REACH + 1
     window_count = span * row_tiles
 
+    toward = 1 - 2 * (position % 2)
     live_mask = tile_cols >= 0
-    offset = jnp.mod(tile_cols // row_tiles - position + REACH, loop_size)
-    local_index = jnp.where(live_mask, offset * row_tiles + tile_cols % row_tiles, -1)
+    offset = jnp.mod(tile_cols // row_tiles - position + REACH, loop_size) - REACH
+    relative = offset * toward
+    order = jnp.where(relative >= 0, relative, REACH - relative)
+    local_index = jnp.where(live_mask, order * row_tiles + tile_cols % row_tiles, -1)
     dense = dense_block(local_index, tile_values, window_count)
     blocks = [dense[:, k * row_count:(k + 1) * row_count] for k in range(span)]
 
     projected = jnp.dot(features, weight, preferred_element_type=jnp.float32).astype(jnp.bfloat16)
-    slabs = []
-    for k in range(span):
-        shift = k - REACH
-        slabs.append(projected if shift == 0 else passed_along(projected, "blk", -shift))
+    slabs = [
+        projected,
+        paired(projected, "blk", 1, -1),
+        paired(projected, "blk", -2, 2),
+        paired(projected, "blk", -1, 1),
+        paired(projected, "blk", 2, -2),
+    ]
 
-    partial_value = jnp.dot(blocks[REACH], slabs[REACH], preferred_element_type=jnp.float32)
-    for k in range(span):
-        if k != REACH:
-            partial_value = partial_value + jnp.dot(blocks[k], slabs[k], preferred_element_type=jnp.float32)
-    partial_value = partial_value.astype(jnp.bfloat16)
-    preact = (
-        partial_value.astype(jnp.float32) + swapped(partial_value, "rep").astype(jnp.float32)
-    ) + bias
+    partial_value = jnp.dot(blocks[0], slabs[0], preferred_element_type=jnp.float32)
+    for k in range(1, span):
+        partial_value = partial_value + jnp.dot(blocks[k], slabs[k], preferred_element_type=jnp.float32)
+    preact = (partial_value + swapped(partial_value, "rep")) + bias
     output, scaled = activate(preact, train_mask, cotangent)
 
     contract_rows = (((0,), (0,)), ((), ()))
-    gathered_sum = lax.dot_general(
-        scaled, blocks[REACH], contract_rows, preferred_element_type=jnp.float32
-    )
-    for k in range(span):
-        shift = k - REACH
-        if shift != 0:
-            piece = lax.dot_general(scaled, blocks[k], contract_rows, preferred_element_type=jnp.float32)
-            gathered_sum = gathered_sum + passed_along(piece.astype(jnp.bfloat16), "blk", shift).astype(
-                jnp.float32
-            )
-    gathered_sum = gathered_sum.astype(jnp.bfloat16)
-    back_sum_t = (
-        gathered_sum.astype(jnp.float32) + swapped(gathered_sum, "rep").astype(jnp.float32)
-    ).astype(jnp.bfloat16)
+    pieces = [
+        lax.dot_general(scaled, blocks[k], contract_rows, preferred_element_type=jnp.float32)
+        for k in range(span)
+    ]
+    from_partner = paired(jnp.stack([pieces[1], pieces[2]]), "blk", 1, -1)
+    far = paired(pieces[4], "blk", -2, 2)
+    near = paired(pieces[3] + from_partner[1], "blk", -1, 1)
+    gathered_sum = pieces[0] + from_partner[0] + near + far
+    back_sum_t = (gathered_sum + swapped(gathered_sum, "rep")).astype(jnp.bfloat16)
     grad_in = lax.dot_general(
         back_sum_t, weight, (((0,), (1,)), ((), ())), preferred_element_type=jnp.float32
     ).astype(jnp.bfloat16)

time: 93.2 us -> 115 us (1.23)
  the two profiles are of different devices: /device:TPU:1 before, /device:TPU:0 now
where the time goes in v5:
time: 115 us; the launch traced here: 114 us
  waiting for transfers between devices  65.4 us (57%)
  starting transfers between devices  22 us (19%)
  matrix products  13.5 us (12%)
  Pallas kernels  8.14 us (7%)
  other arithmetic  3.34 us (3%)
    ppermute x2, waiting for transfers between devices, swapped(): return lax.ppermute(array, axis, [(i, i ^ 1) for i in range(count)])  43.2 us
    ppermute x7, waiting for transfers between devices, paired(): lax.ppermute(array, axis, [(i, (i + (even_by if i % 2 == 0 else odd_by))...  22.2 us
    ppermute x7, starting transfers between devices, paired(): lax.ppermute(array, axis, [(i, (i + (even_by if i % 2 == 0 else odd_by))...  14.3 us
    pallas_call x1, Pallas kernels, dense_block(): pl.pallas_call(kernel, grid_spec=pltpu.PrefetchScalarGridSpec(num_scalar_...  8.14 us
    ppermute x2, starting transfers between devices, swapped(): return lax.ppermute(array, axis, [(i, i ^ 1) for i in range(count)])  7.68 us
    dot_general x4, matrix products, shards(): jnp.dot(blocks[k], slabs[k], preferred_element_type=jnp.float32)  4.99 us
    dot_general x5, matrix products, shards(): lax.dot_general(scaled, blocks[k], contract_rows, preferred_element_type=...  3.66 us
    dot_general x1, matrix products, shards(): jnp.dot(blocks[0], slabs[0], preferred_element_type=jnp.float32)  2.45 us
  transfers between devices with their start and end apart: 9, of which 5 were waited for; matrix products, arithmetic and copies ran while one was open for 9% of the time, Pallas kernels for 7%

profile of v5, /device:TPU:0, one launch (start us, length us, event | category | flops | bytes accessed | tf_op | source)
XLA Modules:
  0.0 114.2 jit_solution(7842462798728964871)
XLA Ops:
  0.6 0.0 copy-start
  0.6 1.0 copy-done
  1.7 1.2 %convolution_convert_fusion.1 = bf16[1024,256]{1,0:T(8,128)(2,1)S(1)} fusion(bf16[1024,256]{1,0:T(8,128)(2,1)S(1)} %copy-done, bf16[256,256]{1,0:T(8,128)(2,1)} %param.8), kind=kOutput, calls=%fused_computation.28 | convolution fusion | flops 134479872 | bytes 1179648 | tf_op jit(solution)/shard_map/dot_general | solution.py:85
  2.9 1.7 %collective-permute-start.3 = (bf16[1024,256]{1,0:T(8,128)(2,1)S(1)}, bf16[1024,256]{1,0:T(8,128)(2,1)S(1)}, u32[]{:S(2)}, u32[]{:S(2)}) collective-permute-start(bf16[1024,256]{1,0:T(8,128)(2,1)S(1)} %convolution_convert_fusion.1), channel_id=1, source_target_pairs={{0,4},{2,126},{4,8},{6,2},{8,12},{10,6},{12,16},{14,10},{16,20},{1... | collective-permute-start | bytes 1572872 | tf_op jit(solution)/shard_map/ppermute | solution.py:18
  4.6 4.9 %collective-permute-start.2 = (bf16[1024,256]{1,0:T(8,128)(2,1)S(1)}, bf16[1024,256]{1,0:T(8,128)(2,1)S(1)}, u32[]{:S(2)}, u32[]{:S(2)}) collective-permute-start(bf16[1024,256]{1,0:T(8,128)(2,1)S(1)} %convolution_convert_fusion.1), channel_id=1, source_target_pairs={{0,126},{2,4},{4,2},{6,8},{8,6},{10,12},{12,10},{14,16},{16,14},{1... | collective-permute-start | bytes 1572872 | tf_op jit(solution)/shard_map/ppermute | solution.py:18
  9.5 0.5 collective-permute-start.1
  9.9 0.0 collective-permute-start
  9.9 1.3 %fusion.48.index_ref = s32[8,8]{1,0:T(8,128)} fusion(s32[8,8]{1,0:T(8,128)} %param.12, s32[]{:T(128)S(6)} %sub.28, s32[]{:T(128)S(6)} %axis_index.15), kind=kLoop, calls=%fused_computation.55 | loop fusion | flops 2624 | bytes 520 | tf_op jit(solution)/shard_map/jit(_where)/select_n | solution.py:81
  11.2 8.1 %shard_map.86 = bf16[1024,5120]{1,0:T(8,128)(2,1)} custom-call(s32[8,8]{1,0:T(8,128)} %fusion.48.index_ref, bf16[8,8,128,128]{3,2,1,0:T(8,128)(2,1)} %values_ref.1), custom_call_target="tpu_custom_call" | custom-call | tf_op jit(solution)/shard_map/pallas_call | solution.py:55
  19.4 0.0 copy-start.1
  19.4 2.5 %fusion.18 = f32[1024,256]{1,0:T(8,128)S(1)} fusion(bf16[1024,256]{1,0:T(8,128)(2,1)S(1)} %convolution_convert_fusion.1, bf16[1024,5120]{1,0:T(8,128)(2,1)} %shard_map.86), kind=kOutput, calls=%fused_computation.19 | convolution fusion | flops 536870912 | bytes 3670016 | tf_op jit(solution)/shard_map/dot_general | solution.py:94
  21.8 0.0 collective-permute-done.3
  21.9 2.8 %fusion.2 = f32[1024,256]{1,0:T(8,128)S(1)} fusion(bf16[1024,256]{1,0:T(8,128)(2,1)S(1)} %collective-permute-done.3, bf16[1024,5120]{1,0:T(8,128)(2,1)} %shard_map.86), kind=kOutput, calls=%fused_computation.3 | convolution fusion | flops 536870912 | bytes 3670016 | tf_op jit(solution)/shard_map/dot_general | solution.py:96
  24.7 0.0 collective-permute-done.2
  24.7 0.0 copy-done.1
  24.7 0.7 fusion.6
  25.5 0.9 collective-permute-done.1
  26.4 0.7 fusion.10
  27.1 0.0 copy-start.4
  27.1 0.0 copy-start.2
  27.1 0.0 copy-start.5
  27.1 0.0 collective-permute-done
  27.2 0.7 fusion.35
  27.9 3.7 %collective-permute-start.4 = (f32[1024,256]{1,0:T(8,128)S(1)}, f32[1024,256]{1,0:T(8,128)S(1)}, u32[]{:S(2)}, u32[]{:S(2)}) collective-permute-start(f32[1024,256]{1,0:T(8,128)S(1)} %fusion.35), channel_id=1, source_target_pairs={{0,1},{1,0},{2,3},{3,2},{4,5},{5,4},{6,7},{7,6},{8,9},{9,8},{10,11... | collective-permute-start | bytes 3145736 | tf_op jit(solution)/shard_map/ppermute | solution.py:25
  31.6 0.0 copy-done.4
  31.6 23.3 %collective-permute-done.4 = f32[1024,256]{1,0:T(8,128)S(1)} collective-permute-done((f32[1024,256]{1,0:T(8,128)S(1)}, f32[1024,256]{1,0:T(8,128)S(1)}, u32[]{:S(2)}, u32[]{:S(2)}) %collective-permute-start.4) | collective-permute-done | bytes 1048608 | tf_op jit(solution)/shard_map/ppermute | solution.py:25
  54.9 0.0 copy-done.2
  54.9 0.0 copy-done.5
  54.9 1.3 %multiply_convert_fusion = (bf16[1024,256]{1,0:T(8,128)(2,1)S(1)}, bf16[1024,256]{1,0:T(8,128)(2,1)}) fusion(bf16[1024,256]{1,0:T(8,128)(2,1)S(1)} %copy-done.2, f32[1024]{0:T(1024)S(1)} %convert_element_type.23, f32[256]{0:T(256)S(1)} %copy-done.5, f32[1024,256]{1,0:T(8,128)S(1)} %fusion.35, f32[1024,256]{1,0:T(8,128)S(1)} %collective-permute-done.4), kind=kLoop, calls=%fused_computation.36 | loop fusion | flops 3932160 | bytes 3675136 | tf_op jit(solution)/shard_map/convert_element_type | solution.py:37
  56.2 0.7 fusion.23
  57.0 0.7 fusion.20
  57.7 0.2 pad_maximum_fusion
  57.9 0.6 collective-permute-start.5
  58.5 0.7 fusion
  59.2 3.5 %collective-permute-start.7 = (f32[256,1024]{1,0:T(8,128)S(1)}, f32[256,1024]{1,0:T(8,128)S(1)}, u32[]{:S(2)}, u32[]{:S(2)}) collective-permute-start(f32[256,1024]{1,0:T(8,128)S(1)} %fusion), channel_id=1, source_target_pairs={{0,124},{2,6},{4,0},{6,10},{8,4},{10,14},{12,8},{14,18},{16,12},{1... | collective-permute-start | bytes 3145736 | tf_op jit(solution)/shard_map/ppermute | solution.py:18
  62.7 0.0 collective-permute-done.5
  62.7 0.7 fusion.38
  63.4 3.2 %collective-permute-start.6 = (f32[256,1024]{1,0:T(8,128)S(1)}, f32[256,1024]{1,0:T(8,128)S(1)}, u32[]{:S(2)}, u32[]{:S(2)}) collective-permute-start(f32[256,1024]{1,0:T(8,128)S(1)} %fusion.38), channel_id=1, source_target_pairs={{0,126},{2,4},{4,2},{6,8},{8,6},{10,12},{12,10},{14,16},{16,14},{1... | collective-permute-start | bytes 3145736 | tf_op jit(solution)/shard_map/ppermute | solution.py:18
  66.6 0.7 fusion.16
  67.3 0.0 copy-start.3
  67.4 7.7 %collective-permute-done.7 = f32[256,1024]{1,0:T(8,128)S(1)} collective-permute-done((f32[256,1024]{1,0:T(8,128)S(1)}, f32[256,1024]{1,0:T(8,128)S(1)}, u32[]{:S(2)}, u32[]{:S(2)}) %collective-permute-start.7) | collective-permute-done | bytes 1048608 | tf_op jit(solution)/shard_map/ppermute | solution.py:18
  75.0 13.6 %collective-permute-done.6 = f32[256,1024]{1,0:T(8,128)S(1)} collective-permute-done((f32[256,1024]{1,0:T(8,128)S(1)}, f32[256,1024]{1,0:T(8,128)S(1)}, u32[]{:S(2)}, u32[]{:S(2)}) %collective-permute-start.6) | collective-permute-done | bytes 1048608 | tf_op jit(solution)/shard_map/ppermute | solution.py:18
  88.6 0.5 fusion.41
  89.1 4.0 %collective-permute-start.8 = (f32[256,1024]{1,0:T(8,128)S(1)}, f32[256,1024]{1,0:T(8,128)S(1)}, u32[]{:S(2)}, u32[]{:S(2)}) collective-permute-start(f32[256,1024]{1,0:T(8,128)S(1)} %fusion.41), channel_id=1, source_target_pairs={{0,1},{1,0},{2,3},{3,2},{4,5},{5,4},{6,7},{7,6},{8,9},{9,8},{10,11... | collective-permute-start | bytes 3145736 | tf_op jit(solution)/shard_map/ppermute | solution.py:25
  93.1 19.9 %collective-permute-done.8 = f32[256,1024]{1,0:T(8,128)S(1)} collective-permute-done((f32[256,1024]{1,0:T(8,128)S(1)}, f32[256,1024]{1,0:T(8,128)S(1)}, u32[]{:S(2)}, u32[]{:S(2)}) %collective-permute-start.8) | collective-permute-done | bytes 1048608 | tf_op jit(solution)/shard_map/ppermute | solution.py:25
  113.0 0.0 copy-done.3
  113.0 1.3 %convolution_convert_fusion = bf16[1024,256]{1,0:T(8,128)(2,1)} fusion(bf16[256,256]{1,0:T(8,128)(2,1)S(1)} %copy-done.3, f32[256,1024]{1,0:T(8,128)S(1)} %fusion.41, f32[256,1024]{1,0:T(8,128)S(1)} %collective-permute-done.8), kind=kOutput, calls=%fused_computation.27 | convolution fusion | flops 135004160 | bytes 2752512 | tf_op jit(solution)/shard_map/dot_general | solution.py:110
  (1 shorter events, 0.0 us)
Async XLA Ops:
  0.6 1.0 copy-start
  2.9 19.0 %collective-permute-start.3 = (bf16[1024,256]{1,0:T(8,128)(2,1)S(1)}, bf16[1024,256]{1,0:T(8,128)(2,1)S(1)}, u32[]{:S(2)}, u32[]{:S(2)}) collective-permute-start(bf16[1024,256]{1,0:T(8,128)(2,1)S(1)} %convolution_convert_fusion.1), channel_id=1, source_target_pairs={{0,4},{2,126},{4,8},{6,2},{8,12},{10,6},{12,16},{14,10},{16,20},{1... | collective-permute-start | bytes 1572872 | tf_op jit(solution)/shard_map/ppermute | solution.py:18
  4.6 20.1 %collective-permute-start.2 = (bf16[1024,256]{1,0:T(8,128)(2,1)S(1)}, bf16[1024,256]{1,0:T(8,128)(2,1)S(1)}, u32[]{:S(2)}, u32[]{:S(2)}) collective-permute-start(bf16[1024,256]{1,0:T(8,128)(2,1)S(1)} %convolution_convert_fusion.1), channel_id=1, source_target_pairs={{0,126},{2,4},{4,2},{6,8},{8,6},{10,12},{12,10},{14,16},{16,14},{1... | collective-permute-start | bytes 1572872 | tf_op jit(solution)/shard_map/ppermute | solution.py:18
  9.5 16.9 %collective-permute-start.1 = (bf16[1024,256]{1,0:T(8,128)(2,1)S(1)}, bf16[1024,256]{1,0:T(8,128)(2,1)S(1)}, u32[]{:S(2)}, u32[]{:S(2)}) collective-permute-start(bf16[1024,256]{1,0:T(8,128)(2,1)S(1)} %convolution_convert_fusion.1), channel_id=1, source_target_pairs={{0,124},{2,6},{4,0},{6,10},{8,4},{10,14},{12,8},{14,18},{16,12},{1... | collective-permute-start | bytes 1572872 | tf_op jit(solution)/shard_map/ppermute | solution.py:18
  9.9 17.2 %collective-permute-start = (bf16[1024,256]{1,0:T(8,128)(2,1)S(1)}, bf16[1024,256]{1,0:T(8,128)(2,1)S(1)}, u32[]{:S(2)}, u32[]{:S(2)}) collective-permute-start(bf16[1024,256]{1,0:T(8,128)(2,1)S(1)} %convolution_convert_fusion.1), channel_id=1, source_target_pairs={{0,2},{2,0},{4,6},{6,4},{8,10},{10,8},{12,14},{14,12},{16,18},{18,... | collective-permute-start | bytes 1572872 | tf_op jit(solution)/shard_map/ppermute | solution.py:18
  19.4 5.3 %copy-start.1 = (bf16[1024,5120]{1,0:T(8,128)(2,1)S(1)}, bf16[1024,5120]{1,0:T(8,128)(2,1)}, u32[]{:S(2)}) copy-start(bf16[1024,5120]{1,0:T(8,128)(2,1)} %shard_map.86) | copy-start | bytes 31457284
  27.1 4.4 %copy-start.4 = (s32[1024]{0:T(1024)S(1)}, s32[1024]{0:T(1024)}, u32[]{:S(2)}) copy-start(s32[1024]{0:T(1024)} %param.11) | copy-start | bytes 12292
  27.1 27.8 %copy-start.2 = (bf16[1024,256]{1,0:T(8,128)(2,1)S(1)}, bf16[1024,256]{1,0:T(8,128)(2,1)}, u32[]{:S(2)}) copy-start(bf16[1024,256]{1,0:T(8,128)(2,1)} %param.10) | copy-start | bytes 1572868
  27.1 27.8 %copy-start.5 = (f32[256]{0:T(256)S(1)}, f32[256]{0:T(256)}, u32[]{:S(2)}) copy-start(f32[256]{0:T(256)} %param.9) | copy-start | bytes 3076
  27.9 27.0 %collective-permute-start.4 = (f32[1024,256]{1,0:T(8,128)S(1)}, f32[1024,256]{1,0:T(8,128)S(1)}, u32[]{:S(2)}, u32[]{:S(2)}) collective-permute-start(f32[1024,256]{1,0:T(8,128)S(1)} %fusion.35), channel_id=1, source_target_pairs={{0,1},{1,0},{2,3},{3,2},{4,5},{5,4},{6,7},{7,6},{8,9},{9,8},{10,11... | collective-permute-start | bytes 3145736 | tf_op jit(solution)/shard_map/ppermute | solution.py:25
  57.9 4.8 %collective-permute-start.5 = (f32[2,256,1024]{2,1,0:T(8,128)S(1)}, f32[2,256,1024]{2,1,0:T(8,128)S(1)}, u32[]{:S(2)}, u32[]{:S(2)}) collective-permute-start(f32[2,256,1024]{2,1,0:T(8,128)S(1)} %pad_maximum_fusion), channel_id=1, source_target_pairs={{0,2},{2,0},{4,6},{6,4},{8,10},{10,8},{12,14},{14,12},{16,18},{18,... | collective-permute-start | bytes 6291464 | tf_op jit(solution)/shard_map/ppermute | solution.py:18
  59.2 15.8 %collective-permute-start.7 = (f32[256,1024]{1,0:T(8,128)S(1)}, f32[256,1024]{1,0:T(8,128)S(1)}, u32[]{:S(2)}, u32[]{:S(2)}) collective-permute-start(f32[256,1024]{1,0:T(8,128)S(1)} %fusion), channel_id=1, source_target_pairs={{0,124},{2,6},{4,0},{6,10},{8,4},{10,14},{12,8},{14,18},{16,12},{1... | collective-permute-start | bytes 3145736 | tf_op jit(solution)/shard_map/ppermute | solution.py:18
  63.4 25.1 %collective-permute-start.6 = (f32[256,1024]{1,0:T(8,128)S(1)}, f32[256,1024]{1,0:T(8,128)S(1)}, u32[]{:S(2)}, u32[]{:S(2)}) collective-permute-start(f32[256,1024]{1,0:T(8,128)S(1)} %fusion.38), channel_id=1, source_target_pairs={{0,126},{2,4},{4,2},{6,8},{8,6},{10,12},{12,10},{14,16},{16,14},{1... | collective-permute-start | bytes 3145736 | tf_op jit(solution)/shard_map/ppermute | solution.py:18
  67.3 45.6 %copy-start.3 = (bf16[256,256]{1,0:T(8,128)(2,1)S(1)}, bf16[256,256]{1,0:T(8,128)(2,1)}, u32[]{:S(2)}) copy-start(bf16[256,256]{1,0:T(8,128)(2,1)} %param.8) | copy-start | bytes 393220
  89.1 23.9 %collective-permute-start.8 = (f32[256,1024]{1,0:T(8,128)S(1)}, f32[256,1024]{1,0:T(8,128)S(1)}, u32[]{:S(2)}, u32[]{:S(2)}) collective-permute-start(f32[256,1024]{1,0:T(8,128)S(1)} %fusion.41), channel_id=1, source_target_pairs={{0,1},{1,0},{2,3},{3,2},{4,5},{5,4},{6,7},{7,6},{8,9},{9,8},{10,11... | collective-permute-start | bytes 3145736 | tf_op jit(solution)/shard_map/ppermute | solution.py:25

commit v6 on v5

--- a/solution.py
+++ b/solution.py
@@ -100,16 +100,27 @@
     contract_rows = (((0,), (0,)), ((), ()))
     pieces = [
         lax.dot_general(scaled, blocks[k], contract_rows, preferred_element_type=jnp.float32)
-        for k in range(span)
+        for k in (0, 3, 4)
     ]
-    from_partner = paired(jnp.stack([pieces[1], pieces[2]]), "blk", 1, -1)
-    far = paired(pieces[4], "blk", -2, 2)
-    near = paired(pieces[3] + from_partner[1], "blk", -1, 1)
-    gathered_sum = pieces[0] + from_partner[0] + near + far
-    back_sum_t = (gathered_sum + swapped(gathered_sum, "rep")).astype(jnp.bfloat16)
-    grad_in = lax.dot_general(
-        back_sum_t, weight, (((0,), (1,)), ((), ())), preferred_element_type=jnp.float32
+    partner_pieces = lax.dot_general(
+        scaled, dense[:, row_count:3 * row_count], contract_rows, preferred_element_type=jnp.float32
+    )
+    from_partner = paired(partner_pieces, "blk", 1, -1)
+    far = paired(pieces[2], "blk", -2, 2)
+    near = paired(pieces[1] + from_partner[:, row_count:], "blk", -1, 1)
+    gathered_sum = pieces[0] + from_partner[:, :row_count] + near + far
+    half_rows = row_count // 2
+    side = lax.axis_index("rep")
+    kept = lax.dynamic_slice_in_dim(gathered_sum, side * half_rows, half_rows, axis=1)
+    sent = lax.dynamic_slice_in_dim(gathered_sum, (1 - side) * half_rows, half_rows, axis=1)
+    back_half = (kept + swapped(sent, "rep")).astype(jnp.bfloat16)
+    own_grad = lax.dot_general(
+        back_half, weight, (((0,), (1,)), ((), ())), preferred_element_type=jnp.float32
     ).astype(jnp.bfloat16)
+    other_grad = swapped(own_grad, "rep")
+    grad_in = jnp.concatenate(
+        [jnp.where(side == 0, own_grad, other_grad), jnp.where(side == 0, other_grad, own_grad)], axis=0
+    )
     return (output, grad_in)
 
 

time: 115 us -> 113 us (0.983)
  waiting for transfers between devices: 65.4 us -> 57.3 us
  matrix products: 13.5 us -> 16.1 us
  starting transfers between devices: 22 us -> 24.2 us
  other arithmetic: 3.34 us -> 5.15 us
    ppermute x2 -> x3, waiting for transfers between devices: 43.2 us -> 36.6 us  [swapped(): return lax.ppermute(array, axis, [(i, i ^ 1) for i in range(count)])]
    ppermute x2 -> x3, starting transfers between devices: 7.68 us -> 10.9 us  [swapped(): return lax.ppermute(array, axis, [(i, i ^ 1) for i in range(count)])]
    dot_general x5 -> x3, matrix products: 3.66 us -> 5.94 us  [shards(): lax.dot_general(scaled, blocks[k], contract_rows, preferred_element_type=...]
    ppermute x7, waiting for transfers between devices: 22.2 us -> 20.8 us  [paired(): lax.ppermute(array, axis, [(i, (i + (even_by if i % 2 == 0 else odd_by))...]
    add x1, other arithmetic: 0.48 us -> 1.63 us  [shards(): gathered_sum = pieces[0] + from_partner[:, :row_count] + near + far]
  transfers between devices with their start and end apart: 9 -> 10, of which waited for: 5 -> 6; matrix products, arithmetic and copies ran while one was open for 9% -> 12% of each run, Pallas kernels for 7% -> 7%
where the time goes in v6:
time: 113 us
  waiting for transfers between devices  57.3 us (51%)
  starting transfers between devices  24.2 us (21%)
  matrix products  16.1 us (14%)
  Pallas kernels  8.14 us (7%)
  other arithmetic  5.15 us (5%)
    ppermute x3, waiting for transfers between devices, swapped(): return lax.ppermute(array, axis, [(i, i ^ 1) for i in range(count)])  36.6 us
    ppermute x7, waiting for transfers between devices, paired(): lax.ppermute(array, axis, [(i, (i + (even_by if i % 2 == 0 else odd_by))...  20.8 us
    ppermute x7, starting transfers between devices, paired(): lax.ppermute(array, axis, [(i, (i + (even_by if i % 2 == 0 else odd_by))...  13.2 us
    ppermute x3, starting transfers between devices, swapped(): return lax.ppermute(array, axis, [(i, i ^ 1) for i in range(count)])  10.9 us
    pallas_call x1, Pallas kernels, dense_block(): pl.pallas_call(kernel, grid_spec=pltpu.PrefetchScalarGridSpec(num_scalar_...  8.14 us
    dot_general x3, matrix products, shards(): lax.dot_general(scaled, blocks[k], contract_rows, preferred_element_type=...  5.94 us
    dot_general x4, matrix products, shards(): jnp.dot(blocks[k], slabs[k], preferred_element_type=jnp.float32)  4.99 us
    dot_general x1, matrix products, shards(): jnp.dot(blocks[0], slabs[0], preferred_element_type=jnp.float32)  2.45 us
  transfers between devices with their start and end apart: 10, of which 6 were waited for; matrix products, arithmetic and copies ran while one was open for 12% of the time, Pallas kernels for 7%

profile of v6, /device:TPU:0, one launch (start us, length us, event | category | flops | bytes accessed | tf_op | source)
XLA Modules:
  0.0 112.8 jit_solution(5256883454090383027)
XLA Ops:
  0.6 0.0 copy-start
  0.6 1.0 copy-done
  1.7 1.2 %convolution_convert_fusion = bf16[1024,256]{1,0:T(8,128)(2,1)S(1)} fusion(bf16[1024,256]{1,0:T(8,128)(2,1)S(1)} %copy-done, bf16[256,256]{1,0:T(8,128)(2,1)} %param.8), kind=kOutput, calls=%fused_computation.22 | convolution fusion | flops 134479872 | bytes 1179648 | tf_op jit(solution)/shard_map/dot_general | solution.py:85
  2.9 1.7 %collective-permute-start.3 = (bf16[1024,256]{1,0:T(8,128)(2,1)S(1)}, bf16[1024,256]{1,0:T(8,128)(2,1)S(1)}, u32[]{:S(2)}, u32[]{:S(2)}) collective-permute-start(bf16[1024,256]{1,0:T(8,128)(2,1)S(1)} %convolution_convert_fusion), channel_id=1, source_target_pairs={{0,4},{2,126},{4,8},{6,2},{8,12},{10,6},{12,16},{14,10},{16,20},{1... | collective-permute-start | bytes 1572872 | tf_op jit(solution)/shard_map/ppermute | solution.py:18
  4.6 4.9 %collective-permute-start.2 = (bf16[1024,256]{1,0:T(8,128)(2,1)S(1)}, bf16[1024,256]{1,0:T(8,128)(2,1)S(1)}, u32[]{:S(2)}, u32[]{:S(2)}) collective-permute-start(bf16[1024,256]{1,0:T(8,128)(2,1)S(1)} %convolution_convert_fusion), channel_id=1, source_target_pairs={{0,126},{2,4},{4,2},{6,8},{8,6},{10,12},{12,10},{14,16},{16,14},{1... | collective-permute-start | bytes 1572872 | tf_op jit(solution)/shard_map/ppermute | solution.py:18
  9.5 0.5 collective-permute-start.1
  9.9 0.0 collective-permute-start
  9.9 1.3 %fusion.38.index_ref = s32[8,8]{1,0:T(8,128)} fusion(s32[8,8]{1,0:T(8,128)} %param.12, s32[]{:T(128)S(6)} %sub.31, s32[]{:T(128)S(6)} %axis_index.23), kind=kLoop, calls=%fused_computation.51 | loop fusion | flops 2624 | bytes 520 | tf_op jit(solution)/shard_map/jit(_where)/select_n | solution.py:81
  11.2 8.1 %shard_map.86 = bf16[1024,5120]{1,0:T(8,128)(2,1)} custom-call(s32[8,8]{1,0:T(8,128)} %fusion.38.index_ref, bf16[8,8,128,128]{3,2,1,0:T(8,128)(2,1)} %values_ref.1), custom_call_target="tpu_custom_call" | custom-call | tf_op jit(solution)/shard_map/pallas_call | solution.py:55
  19.4 2.4 %fusion.16 = f32[1024,256]{1,0:T(8,128)S(1)} fusion(bf16[1024,256]{1,0:T(8,128)(2,1)S(1)} %convolution_convert_fusion, bf16[1024,5120]{1,0:T(8,128)(2,1)} %shard_map.86), kind=kOutput, calls=%fused_computation.16 | convolution fusion | flops 536870912 | bytes 3670016 | tf_op jit(solution)/shard_map/dot_general | solution.py:94
  21.8 0.0 collective-permute-done.3
  21.9 2.8 %fusion.8 = f32[1024,256]{1,0:T(8,128)S(1)} fusion(bf16[1024,256]{1,0:T(8,128)(2,1)S(1)} %collective-permute-done.3, bf16[1024,5120]{1,0:T(8,128)(2,1)} %shard_map.86), kind=kOutput, calls=%fused_computation.8 | convolution fusion | flops 536870912 | bytes 3670016 | tf_op jit(solution)/shard_map/dot_general | solution.py:96
  24.7 0.0 collective-permute-done.2
  24.7 0.0 copy-done.1
  24.7 0.7 fusion.12
  25.5 0.9 collective-permute-done.1
  26.4 0.7 fusion.2
  27.1 0.0 copy-start.6
  27.1 0.0 copy-start.4
  27.1 0.0 copy-start.7
  27.1 0.0 collective-permute-done
  27.2 0.7 fusion.27
  27.9 3.7 %collective-permute-start.4 = (f32[1024,256]{1,0:T(8,128)S(1)}, f32[1024,256]{1,0:T(8,128)S(1)}, u32[]{:S(2)}, u32[]{:S(2)}) collective-permute-start(f32[1024,256]{1,0:T(8,128)S(1)} %fusion.27), channel_id=1, source_target_pairs={{0,1},{1,0},{2,3},{3,2},{4,5},{5,4},{6,7},{7,6},{8,9},{9,8},{10,11... | collective-permute-start | bytes 3145736 | tf_op jit(solution)/shard_map/ppermute | solution.py:25
  31.6 0.0 copy-done.6
  31.6 23.3 %collective-permute-done.4 = f32[1024,256]{1,0:T(8,128)S(1)} collective-permute-done((f32[1024,256]{1,0:T(8,128)S(1)}, f32[1024,256]{1,0:T(8,128)S(1)}, u32[]{:S(2)}, u32[]{:S(2)}) %collective-permute-start.4) | collective-permute-done | bytes 1048608 | tf_op jit(solution)/shard_map/ppermute | solution.py:25
  54.9 0.0 copy-done.4
  54.9 0.0 copy-done.7
  54.9 1.3 %multiply_convert_fusion = (bf16[1024,256]{1,0:T(8,128)(2,1)S(1)}, bf16[1024,256]{1,0:T(8,128)(2,1)}) fusion(bf16[1024,256]{1,0:T(8,128)(2,1)S(1)} %copy-done.4, f32[1024]{0:T(1024)S(1)} %convert_element_type.23, f32[256]{0:T(256)S(1)} %copy-done.7, f32[1024,256]{1,0:T(8,128)S(1)} %fusion.27, f32[1024,256]{1,0:T(8,128)S(1)} %collective-permute-done.4), kind=kLoop, calls=%fused_computation.28 | loop fusion | flops 3932160 | bytes 3675136 | tf_op jit(solution)/shard_map/convert_element_type | solution.py:37
  56.2 1.3 %fusion = f32[256,2048]{1,0:T(8,128)S(1)} fusion(bf16[1024,256]{1,0:T(8,128)(2,1)S(1)} %get-tuple-element.2, bf16[1024,5120]{1,0:T(8,128)(2,1)S(1)} %copy-done.1), kind=kOutput, calls=%fused_computation | convolution fusion | flops 1073741824 | bytes 6815744 | tf_op jit(solution)/shard_map/dot_general | solution.py:105
  57.5 0.6 collective-permute-start.5
  58.1 1.8 %fusion.6 = f32[256,1024]{1,0:T(8,128)} fusion(bf16[1024,256]{1,0:T(8,128)(2,1)S(1)} %get-tuple-element.2, bf16[1024,5120]{1,0:T(8,128)(2,1)S(1)} %copy-done.1), kind=kOutput, calls=%fused_computation.6 | convolution fusion | flops 536870912 | bytes 3670016 | tf_op jit(solution)/shard_map/dot_general | solution.py:102
  59.9 3.4 %collective-permute-start.7 = (f32[256,1024]{1,0:T(8,128)}, f32[256,1024]{1,0:T(8,128)S(1)}, u32[]{:S(2)}, u32[]{:S(2)}) collective-permute-start(f32[256,1024]{1,0:T(8,128)} %fusion.6), channel_id=1, source_target_pairs={{0,124},{2,6},{4,0},{6,10},{8,4},{10,14},{12,8},{14,18},{16,12},{1... | collective-permute-start | bytes 3145736 | tf_op jit(solution)/shard_map/ppermute | solution.py:18
  63.3 0.0 collective-permute-done.5
  63.3 1.7 %slice_add_fusion = f32[256,1024]{1,0:T(8,128)} fusion(f32[256,2048]{1,0:T(8,128)S(1)} %collective-permute-done.5, bf16[1024,256]{1,0:T(8,128)(2,1)S(1)} %get-tuple-element.2, bf16[1024,5120]{1,0:T(8,128)(2,1)S(1)} %copy-done.1), kind=kOutput, calls=%fused_computation.24 | convolution fusion | flops 537133056 | bytes 4718592 | tf_op jit(solution)/shard_map/dot_general | solution.py:102
  65.0 0.0 copy-done.2
  65.0 2.2 %collective-permute-start.6 = (f32[256,1024]{1,0:T(8,128)}, f32[256,1024]{1,0:T(8,128)}, u32[]{:S(2)}, u32[]{:S(2)}) collective-permute-start(f32[256,1024]{1,0:T(8,128)} %slice_add_fusion), channel_id=1, source_target_pairs={{0,126},{2,4},{4,2},{6,8},{8,6},{10,12},{12,10},{14,16},{16,14},{1... | collective-permute-start | bytes 3145736 | tf_op jit(solution)/shard_map/ppermute | solution.py:18
  67.2 2.5 %fusion.14 = f32[256,1024]{1,0:T(8,128)S(1)} fusion(bf16[1024,256]{1,0:T(8,128)(2,1)S(1)} %get-tuple-element.2, bf16[1024,5120]{1,0:T(8,128)(2,1)} %shard_map.86), kind=kOutput, calls=%fused_computation.14 | convolution fusion | flops 536870912 | bytes 3670016 | tf_op jit(solution)/shard_map/dot_general | solution.py:102
  69.6 0.0 copy-start.5
  69.6 6.2 %collective-permute-done.7 = f32[256,1024]{1,0:T(8,128)S(1)} collective-permute-done((f32[256,1024]{1,0:T(8,128)}, f32[256,1024]{1,0:T(8,128)S(1)}, u32[]{:S(2)}, u32[]{:S(2)}) %collective-permute-start.7) | collective-permute-done | bytes 1048608 | tf_op jit(solution)/shard_map/ppermute | solution.py:18
  75.9 13.6 %collective-permute-done.6 = f32[256,1024]{1,0:T(8,128)} collective-permute-done((f32[256,1024]{1,0:T(8,128)}, f32[256,1024]{1,0:T(8,128)}, u32[]{:S(2)}, u32[]{:S(2)}) %collective-permute-start.6) | collective-permute-done | bytes 1048608 | tf_op jit(solution)/shard_map/ppermute | solution.py:18
  89.5 0.0 copy-done.3
  89.5 1.6 %fusion.31 = f32[256,1024]{1,0:T(8,128)S(1)} fusion(f32[256,1024]{1,0:T(8,128)S(1)} %collective-permute-done.7, f32[256,1024]{1,0:T(8,128)} %collective-permute-done.6, f32[256,1024]{1,0:T(8,128)S(1)} %fusion.14, f32[256,2048]{1,0:T(8,128)S(1)} %copy-done.3), kind=kLoop, calls=%fused_computation.27 | loop fusion | flops 786432 | bytes 5242880 | tf_op jit(solution)/shard_map/add | solution.py:111
  91.2 3.9 %collective-permute-start.8 = (f32[256,512]{1,0:T(8,128)S(1)}, f32[256,512]{1,0:T(8,128)S(1)}, u32[]{:S(2)}, u32[]{:S(2)}) collective-permute-start(f32[256,512]{1,0:T(8,128)S(1)} %constant_dynamic-slice_fusion), channel_id=1, source_target_pairs={{0,1},{1,0},{2,3},{3,2},{4,5},{5,4},{6,7},{7,6},{8,9},{9,8},{10,11... | collective-permute-start | bytes 1572872 | tf_op jit(solution)/shard_map/ppermute | solution.py:25
  95.1 8.6 %collective-permute-done.8 = f32[256,512]{1,0:T(8,128)S(1)} collective-permute-done((f32[256,512]{1,0:T(8,128)S(1)}, f32[256,512]{1,0:T(8,128)S(1)}, u32[]{:S(2)}, u32[]{:S(2)}) %collective-permute-start.8) | collective-permute-done | bytes 524320 | tf_op jit(solution)/shard_map/ppermute | solution.py:25
  103.7 0.3 convolution_convert_fusion.1
  104.0 3.3 %collective-permute-start.9 = (bf16[512,256]{1,0:T(8,128)(2,1)S(1)}, bf16[512,256]{1,0:T(8,128)(2,1)S(1)}, u32[]{:S(2)}, u32[]{:S(2)}) collective-permute-start(bf16[512,256]{1,0:T(8,128)(2,1)S(1)} %convolution_convert_fusion.1), channel_id=1, source_target_pairs={{0,1},{1,0},{2,3},{3,2},{4,5},{5,4},{6,7},{7,6},{8,9},{9,8},{10,11... | collective-permute-start | bytes 786440 | tf_op jit(solution)/shard_map/ppermute | solution.py:25
  107.3 4.6 %collective-permute-done.9 = bf16[512,256]{1,0:T(8,128)(2,1)S(1)} collective-permute-done((bf16[512,256]{1,0:T(8,128)(2,1)S(1)}, bf16[512,256]{1,0:T(8,128)(2,1)S(1)}, u32[]{:S(2)}, u32[]{:S(2)}) %collective-permute-start.9) | collective-permute-done | bytes 262176 | tf_op jit(solution)/shard_map/ppermute | solution.py:25
  112.0 0.8 pad_maximum_fusion
  (7 shorter events, 0.1 us)
Async XLA Ops:
  0.6 1.0 copy-start
  2.9 19.0 %collective-permute-start.3 = (bf16[1024,256]{1,0:T(8,128)(2,1)S(1)}, bf16[1024,256]{1,0:T(8,128)(2,1)S(1)}, u32[]{:S(2)}, u32[]{:S(2)}) collective-permute-start(bf16[1024,256]{1,0:T(8,128)(2,1)S(1)} %convolution_convert_fusion), channel_id=1, source_target_pairs={{0,4},{2,126},{4,8},{6,2},{8,12},{10,6},{12,16},{14,10},{16,20},{1... | collective-permute-start | bytes 1572872 | tf_op jit(solution)/shard_map/ppermute | solution.py:18
  4.6 20.1 %collective-permute-start.2 = (bf16[1024,256]{1,0:T(8,128)(2,1)S(1)}, bf16[1024,256]{1,0:T(8,128)(2,1)S(1)}, u32[]{:S(2)}, u32[]{:S(2)}) collective-permute-start(bf16[1024,256]{1,0:T(8,128)(2,1)S(1)} %convolution_convert_fusion), channel_id=1, source_target_pairs={{0,126},{2,4},{4,2},{6,8},{8,6},{10,12},{12,10},{14,16},{16,14},{1... | collective-permute-start | bytes 1572872 | tf_op jit(solution)/shard_map/ppermute | solution.py:18
  9.5 16.9 %collective-permute-start.1 = (bf16[1024,256]{1,0:T(8,128)(2,1)S(1)}, bf16[1024,256]{1,0:T(8,128)(2,1)S(1)}, u32[]{:S(2)}, u32[]{:S(2)}) collective-permute-start(bf16[1024,256]{1,0:T(8,128)(2,1)S(1)} %convolution_convert_fusion), channel_id=1, source_target_pairs={{0,124},{2,6},{4,0},{6,10},{8,4},{10,14},{12,8},{14,18},{16,12},{1... | collective-permute-start | bytes 1572872 | tf_op jit(solution)/shard_map/ppermute | solution.py:18
  9.9 17.2 %collective-permute-start = (bf16[1024,256]{1,0:T(8,128)(2,1)S(1)}, bf16[1024,256]{1,0:T(8,128)(2,1)S(1)}, u32[]{:S(2)}, u32[]{:S(2)}) collective-permute-start(bf16[1024,256]{1,0:T(8,128)(2,1)S(1)} %convolution_convert_fusion), channel_id=1, source_target_pairs={{0,2},{2,0},{4,6},{6,4},{8,10},{10,8},{12,14},{14,12},{16,18},{18,... | collective-permute-start | bytes 1572872 | tf_op jit(solution)/shard_map/ppermute | solution.py:18
  19.4 5.3 %copy-start.1 = (bf16[1024,5120]{1,0:T(8,128)(2,1)S(1)}, bf16[1024,5120]{1,0:T(8,128)(2,1)}, u32[]{:S(2)}) copy-start(bf16[1024,5120]{1,0:T(8,128)(2,1)} %shard_map.86) | copy-start | bytes 31457284
  27.1 4.4 %copy-start.6 = (s32[1024]{0:T(1024)S(1)}, s32[1024]{0:T(1024)}, u32[]{:S(2)}) copy-start(s32[1024]{0:T(1024)} %param.11) | copy-start | bytes 12292
  27.1 27.8 %copy-start.4 = (bf16[1024,256]{1,0:T(8,128)(2,1)S(1)}, bf16[1024,256]{1,0:T(8,128)(2,1)}, u32[]{:S(2)}) copy-start(bf16[1024,256]{1,0:T(8,128)(2,1)} %param.10) | copy-start | bytes 1572868
  27.1 27.8 %copy-start.7 = (f32[256]{0:T(256)S(1)}, f32[256]{0:T(256)}, u32[]{:S(2)}) copy-start(f32[256]{0:T(256)} %param.9) | copy-start | bytes 3076
  27.9 27.0 %collective-permute-start.4 = (f32[1024,256]{1,0:T(8,128)S(1)}, f32[1024,256]{1,0:T(8,128)S(1)}, u32[]{:S(2)}, u32[]{:S(2)}) collective-permute-start(f32[1024,256]{1,0:T(8,128)S(1)} %fusion.27), channel_id=1, source_target_pairs={{0,1},{1,0},{2,3},{3,2},{4,5},{5,4},{6,7},{7,6},{8,9},{9,8},{10,11... | collective-permute-start | bytes 3145736 | tf_op jit(solution)/shard_map/ppermute | solution.py:25
  57.5 5.7 %collective-permute-start.5 = (f32[256,2048]{1,0:T(8,128)S(1)}, f32[256,2048]{1,0:T(8,128)S(1)}, u32[]{:S(2)}, u32[]{:S(2)}) collective-permute-start(f32[256,2048]{1,0:T(8,128)S(1)} %fusion), channel_id=1, source_target_pairs={{0,2},{2,0},{4,6},{6,4},{8,10},{10,8},{12,14},{14,12},{16,18},{18,... | collective-permute-start | bytes 6291464 | tf_op jit(solution)/shard_map/ppermute | solution.py:18
  59.9 16.0 %collective-permute-start.7 = (f32[256,1024]{1,0:T(8,128)}, f32[256,1024]{1,0:T(8,128)S(1)}, u32[]{:S(2)}, u32[]{:S(2)}) collective-permute-start(f32[256,1024]{1,0:T(8,128)} %fusion.6), channel_id=1, source_target_pairs={{0,124},{2,6},{4,0},{6,10},{8,4},{10,14},{12,8},{14,18},{16,12},{1... | collective-permute-start | bytes 3145736 | tf_op jit(solution)/shard_map/ppermute | solution.py:18
  63.3 1.7 %copy-start.2 = (f32[256,2048]{1,0:T(8,128)}, f32[256,2048]{1,0:T(8,128)S(1)}, u32[]{:S(2)}) copy-start(f32[256,2048]{1,0:T(8,128)S(1)} %collective-permute-done.5) | copy-start | bytes 6291460
  65.0 24.5 %collective-permute-start.6 = (f32[256,1024]{1,0:T(8,128)}, f32[256,1024]{1,0:T(8,128)}, u32[]{:S(2)}, u32[]{:S(2)}) collective-permute-start(f32[256,1024]{1,0:T(8,128)} %slice_add_fusion), channel_id=1, source_target_pairs={{0,126},{2,4},{4,2},{6,8},{8,6},{10,12},{12,10},{14,16},{16,14},{1... | collective-permute-start | bytes 3145736 | tf_op jit(solution)/shard_map/ppermute | solution.py:18
  67.2 22.3 %copy-start.3 = (f32[256,2048]{1,0:T(8,128)S(1)}, f32[256,2048]{1,0:T(8,128)}, u32[]{:S(2)}) copy-start(f32[256,2048]{1,0:T(8,128)} %copy-done.2) | copy-start | bytes 6291460
  69.6 34.1 %copy-start.5 = (bf16[256,256]{1,0:T(8,128)(2,1)S(1)}, bf16[256,256]{1,0:T(8,128)(2,1)}, u32[]{:S(2)}) copy-start(bf16[256,256]{1,0:T(8,128)(2,1)} %param.8) | copy-start | bytes 393220
  91.2 12.5 %collective-permute-start.8 = (f32[256,512]{1,0:T(8,128)S(1)}, f32[256,512]{1,0:T(8,128)S(1)}, u32[]{:S(2)}, u32[]{:S(2)}) collective-permute-start(f32[256,512]{1,0:T(8,128)S(1)} %constant_dynamic-slice_fusion), channel_id=1, source_target_pairs={{0,1},{1,0},{2,3},{3,2},{4,5},{5,4},{6,7},{7,6},{8,9},{9,8},{10,11... | collective-permute-start | bytes 1572872 | tf_op jit(solution)/shard_map/ppermute | solution.py:25
  104.0 8.0 %collective-permute-start.9 = (bf16[512,256]{1,0:T(8,128)(2,1)S(1)}, bf16[512,256]{1,0:T(8,128)(2,1)S(1)}, u32[]{:S(2)}, u32[]{:S(2)}) collective-permute-start(bf16[512,256]{1,0:T(8,128)(2,1)S(1)} %convolution_convert_fusion.1), channel_id=1, source_target_pairs={{0,1},{1,0},{2,3},{3,2},{4,5},{5,4},{6,7},{7,6},{8,9},{9,8},{10,11... | collective-permute-start | bytes 786440 | tf_op jit(solution)/shard_map/ppermute | solution.py:25
